TPU v7x, 128 devices: a whole 4x4x4 slice. The times are simulated.
128 devices in a mesh: ang: 4 (over y), pix: 32 (over x, z, core).
Axes of the slice: x: 4, y: 4, z: 4, core: 2. Of those that a mesh axis runs over, the one named last changes fastest.
Arguments:
- flats: float32 [256, 256, 4096], P(None, 'pix', 'ang'), may hold values from -60 to 60
- projections: float32 [128, 256, 4096], P('ang', None, 'pix'), may hold values from -60 to 60
- start_basis: float32 [256, 48], replicated, may hold values from -0.375 to 0.375
Outputs:
- corrected: float32 [128, 256, 4096], P('ang', None, 'pix')
All inputs are finite; a program needn't handle non-finite values.
Results may differ from a plain program's by a relative error of at most 0.0001.
Values sent between devices are 32-bit elements; how exact they have to be, the bound alone decides.
No kernel may reach another device: no remote copies, remote signals or barrier semaphores. Data moves between devices by JAX's collectives and lax.ppermute only.
A program may use at most 128 MiB of HBM per device.

v0:
```python
import jax
import jax.numpy as jnp
from jax import lax
from jax.sharding import PartitionSpec as P
from jax.experimental import pallas as pl

SUBSPACE = 2


floor_value = 0.2


def orthonormal(grown):
    correlation = jnp.dot(grown.T, grown, precision=lax.Precision.HIGHEST)
    lower = jnp.linalg.cholesky(correlation)
    return jax.scipy.linalg.solve_triangular(lower, grown.T, lower=True).T


def solve_normal(normal, fit_rhs):
    factor = jnp.linalg.cholesky(normal)
    return jax.scipy.linalg.cho_solve((factor, True), fit_rhs.T).T


def sum_by_exchange(rows, axes, count):
    total, width = rows.shape
    pieces = lax.all_to_all(rows.reshape(count, total // count, width), axes, 0, 0, tiled=True)
    block = jnp.sum(pieces, axis=0)
    spread = jnp.broadcast_to(block[None], (count,) + block.shape)
    gathered = lax.all_to_all(spread, axes, 0, 0, tiled=True)
    return gathered.reshape(total, width)


def _gram_kernel(flats_ref, gram_ref, mean_ref):
    step = pl.program_id(0)

    @pl.when(step == 0)
    def _():
        gram_ref[...] = jnp.zeros_like(gram_ref)

    block = flats_ref[...]
    mean = jnp.sum(block, axis=0) / block.shape[0]
    mean_ref[...] = mean
    total = gram_ref[...]
    for row in range(block.shape[1]):
        centred = block[:, row, :] - mean[row][None, :]
        total += lax.dot_general(
            centred, centred, (((1,), (1,)), ((), ())),
            precision=lax.Precision.HIGHEST, preferred_element_type=jnp.float32,
        )
    gram_ref[...] = total


def frame_gram(flats, width=256):
    frames, rows, cols = flats.shape
    return pl.pallas_call(
        _gram_kernel,
        grid=(cols // width,),
        in_specs=[pl.BlockSpec((frames, rows, width), lambda i: (0, 0, i))],
        out_specs=[
            pl.BlockSpec((frames, frames), lambda i: (0, 0)),
            pl.BlockSpec((rows, width), lambda i: (0, i)),
        ],
        out_shape=[
            jax.ShapeDtypeStruct((frames, frames), jnp.float32),
            jax.ShapeDtypeStruct((rows, cols), jnp.float32),
        ],
    )(flats)


def _project_kernel(lhs_ref, flats_ref, mean_ref, out_ref):
    lhs = lhs_ref[...]
    for row in range(flats_ref.shape[1]):
        centred = flats_ref[:, row, :] - mean_ref[row, :][None, :]
        out_ref[:, row, :] = jnp.dot(
            lhs, centred, precision=lax.Precision.HIGH,
            preferred_element_type=jnp.float32,
        )


def project_rows(lhs, flats, mean):
    m, k = lhs.shape
    _, rows, width = flats.shape
    return pl.pallas_call(
        _project_kernel,
        grid=(1,),
        in_specs=[
            pl.BlockSpec((m, k), lambda r: (0, 0)),
            pl.BlockSpec((k, rows, width), lambda r: (0, 0, 0)),
            pl.BlockSpec((rows, width), lambda r: (0, 0)),
        ],
        out_specs=pl.BlockSpec((m, rows, width), lambda r: (0, 0, 0)),
        out_shape=jax.ShapeDtypeStruct((m, rows, width), jnp.float32),
    )(lhs, flats, mean)


def shards(flats, projections, start_basis):
    frames_here, rows_dev, cols_dev = flats.shape
    ang_count = lax.axis_size("ang")
    pix_count = lax.axis_size("pix")
    npix = rows_dev * cols_dev * ang_count * pix_count
    angle_count, rows_all, cols_here = projections.shape

    tiles_in = projections.reshape(angle_count, pix_count, rows_dev, cols_here).transpose(1, 0, 2, 3)
    tiles = lax.all_to_all(tiles_in, "pix", 0, 0, tiled=True)

    local_gram, mean_flat = frame_gram(flats)
    device_count = ang_count * pix_count
    gram_rows = local_gram.reshape(device_count, -1)
    gram = sum_by_exchange(gram_rows, ("ang", "pix"), device_count).reshape(frames_here, frames_here) / npix
    basis = start_basis
    for turn in range(SUBSPACE):
        basis = orthonormal(jnp.dot(gram, basis, precision=lax.Precision.HIGHEST))
    eigen_3d = project_rows(basis.T, flats, mean_flat)
    eigen_flats = eigen_3d.reshape(basis.shape[1], -1)
    normal = jnp.dot(
        basis.T,
        jnp.dot(gram, basis, precision=lax.Precision.HIGHEST),
        precision=lax.Precision.HIGHEST,
    )
    eigen_count = eigen_flats.shape[0]
    eigen_rows = lax.all_gather(
        eigen_3d, "ang", axis=2, tiled=True
    )
    mean_rows = lax.all_gather(mean_flat, "ang", axis=1, tiled=True)
    eigen_blk = eigen_rows.reshape(eigen_count, rows_dev, pix_count, cols_here)
    mean_blk = mean_rows.reshape(rows_dev, pix_count, cols_here)
    centred_frames = tiles - mean_blk.transpose(1, 0, 2)[:, None]
    partial_value = jnp.einsum(
        "pjrc,krpc->jk", centred_frames, eigen_blk, precision=lax.Precision.HIGH
    )
    fit_rhs = sum_by_exchange(partial_value, "pix", pix_count) / npix
    weights = solve_normal(normal, fit_rhs)
    estimate = mean_blk.transpose(1, 0, 2)[:, None] + jnp.einsum(
        "jk,krpc->pjrc", weights, eigen_blk, precision=lax.Precision.HIGH
    )
    tiles_out = tiles / jnp.maximum(estimate, floor_value)
    back = lax.all_to_all(tiles_out, "pix", 0, 0, tiled=True)
    result = back.transpose(1, 0, 2, 3).reshape(angle_count, rows_all, cols_here)
    return result


def solution(mesh):
    in_specs = (P(None, "pix", "ang"), P("ang", None, "pix"), P())
    out_specs = P("ang", None, "pix")
    return jax.shard_map(shards, mesh=mesh, in_specs=in_specs, out_specs=out_specs, check_vma=False)
```

profile of v0, /device:TPU:1, one launch (start us, length us, event | category | flops | bytes accessed | tf_op | source)
XLA Modules:
  0.0 269.6 jit_solution(1477346127192300514)
XLA Ops:
  6.5 0.0 copy-start
  6.5 0.0 all-gather.2.cloned.1.call-start
  6.5 13.7 %shard_map.37 = (f32[256,256]{1,0:T(8,128)}, f32[8,1024]{1,0:T(8,128)}) custom-call(f32[256,8,1024]{2,1,0:T(8,128)} %flats_ref.3), custom_call_target="tpu_custom_call" | custom-call | tf_op jit(solution)/shard_map/pallas_call | solution.py:55
  20.2 1.2 reshape_reshape.5
  21.5 22.2 %all_to_all.30 = f32[128,1,512]{2,1,0:T(1,128)S(1)} all-to-all(f32[128,1,512]{2,1,0:T(1,128)S(1)} %reshape_reshape.5), channel_id=1, replica_groups=mesh['ang'=4,'pix'=32] {'ang','pix'}, dimensions={0} | all-to-all | bytes 524288 | tf_op jit(solution)/shard_map/all_to_all | solution.py:26
  43.7 0.2 reduce_sum.18
  43.9 0.1 broadcast_in_dim.4
  44.1 15.2 %all_to_all.31 = f32[128,1,512]{2,1,0:T(1,128)S(1)} all-to-all(f32[128,1,512]{2,1,0:T(1,128)S(1)} %broadcast_in_dim.4), channel_id=1, replica_groups=mesh['ang'=4,'pix'=32] {'ang','pix'}, dimensions={0} | all-to-all | bytes 524288 | tf_op jit(solution)/shard_map/all_to_all | solution.py:29
  59.3 0.7 multiply_reduce_fusion
  60.0 0.0 copy-done
  60.1 0.4 fusion.26
  60.4 0.2 fusion.27
  60.6 0.1 copy.23
  60.7 4.4 %cholesky.59 = f32[48,48]{1,0:T(8,128)S(1)} custom-call(f32[48,48]{1,0:T(8,128)S(1)} %fusion.23), custom_call_target="Cholesky" | custom-call | tf_op jit(solution)/shard_map/jit(cholesky)/cholesky | solution.py:15
  65.1 0.6 compare_reduce_fusion.2
  65.8 0.7 fusion.13
  66.4 3.7 %custom-call.14 = f32[1,48,48]{1,2,0:T(8,128)S(1)} custom-call(f32[1,48,48]{2,1,0:T(8,128)S(1)} %fusion.13), custom_call_target="InvertDiagBlocksLowerTriangular" | custom-call | tf_op jit(solution)/shard_map/jit(_solve_triangular)/triangular_solve | solution.py:16
  70.1 0.2 fusion.11
  70.3 0.4 fusion.28
  70.7 0.2 fusion.29
  70.9 0.1 copy.24
  71.0 4.4 %cholesky.70 = f32[48,48]{1,0:T(8,128)S(1)} custom-call(f32[48,48]{1,0:T(8,128)S(1)} %fusion.21), custom_call_target="Cholesky" | custom-call | tf_op jit(solution)/shard_map/jit(cholesky)/cholesky | solution.py:15
  75.4 0.6 compare_reduce_fusion.1
  76.0 0.7 fusion.14
  76.7 3.7 %custom-call.15 = f32[1,48,48]{1,2,0:T(8,128)S(1)} custom-call(f32[1,48,48]{2,1,0:T(8,128)S(1)} %fusion.14), custom_call_target="InvertDiagBlocksLowerTriangular" | custom-call | tf_op jit(solution)/shard_map/jit(_solve_triangular)/triangular_solve | solution.py:16
  80.4 0.9 fusion.9.lhs_ref
  81.3 9.5 %shard_map.38 = f32[48,8,1024]{2,1,0:T(8,128)} custom-call(f32[48,256]{1,0:T(8,128)} %fusion.9.lhs_ref, f32[256,8,1024]{2,1,0:T(8,128)} %flats_ref.3, f32[8,1024]{1,0:T(8,128)} %get-tuple-element.9.mean_ref), custom_call_target="tpu_custom_call" | custom-call | tf_op jit(solution)/shard_map/pallas_call | solution.py:83
  90.8 0.0 all-gather.2.cloned.1.call-update
  90.8 6.6 %copy.20 = f32[32,32,8,128]{3,1,2,0:T(8,128)} copy(f32[32,32,8,128]{3,2,0,1:T(8,128)} %bitcast.82) | data formatting | bytes 8388608 | tf_op jit(solution)/shard_map/transpose | solution.py:103
  97.4 0.0 copy-start.2
  97.4 0.0 copy-start.1
  97.4 5.7 %all-to-all-start = ((f32[32,32,8,128]{3,1,2,0:T(8,128)}), f32[32,32,8,128]{3,1,2,0:T(8,128)}, u32[]{:S(2)}, u32[]{:S(2)}) async-start(f32[32,32,8,128]{3,1,2,0:T(8,128)} %copy.20), calls=%async_computation | async-start | bytes 8388608 | tf_op jit(solution)/shard_map/all_to_all | solution.py:104
  103.1 0.0 copy-done.2
  103.1 11.0 %all_gather.6 = f32[8,4096]{1,0:T(8,128)S(1)} all-gather(f32[8,1024]{1,0:T(8,128)S(1)} %copy-done.2), channel_id=1, replica_groups=mesh['ang'=4,'pix'=32] {'ang'}, dimensions={1}, use_global_device_ids=true | all-gather | bytes 163840 | tf_op jit(solution)/shard_map/all_gather | solution.py:124
  114.1 0.0 copy-done.1
  114.1 0.4 fusion.30
  114.5 0.2 fusion.31
  114.6 0.1 copy.25
  114.7 4.4 %cholesky.81 = f32[48,48]{1,0:T(8,128)S(1)} custom-call(f32[48,48]{1,0:T(8,128)S(1)} %fusion.19), custom_call_target="Cholesky" | custom-call | tf_op jit(solution)/shard_map/jit(cholesky)/cholesky | solution.py:20
  119.2 36.2 %all-to-all-done = f32[32,32,8,128]{3,1,2,0:T(8,128)} async-done(((f32[32,32,8,128]{3,1,2,0:T(8,128)}), f32[32,32,8,128]{3,1,2,0:T(8,128)}, u32[]{:S(2)}, u32[]{:S(2)}) %all-to-all-start) | async-done | bytes 4194336 | tf_op jit(solution)/shard_map/all_to_all | solution.py:104
  155.4 0.0 all-gather.2.cloned.1.call-done
  155.4 11.1 %fusion.2 = f32[32,48,1,1]{1,0,3,2:T(8,128)} fusion(f32[48,8,32,128]{3,1,2,0:T(8,128)} %bitcast.80, f32[32,32,8,128]{3,1,2,0:T(8,128)} %all-to-all-done, f32[32,8,128]{2,0,1:T(8,128)S(1)} %copy.21), kind=kOutput, calls=%fused_computation.2 | convolution fusion | flops 303038464 | bytes 10622976 | tf_op jit(solution)/shard_map/pjrc,krpc->jk/dot_general | solution.py:128
  166.5 7.1 %all-to-all-start.3 = ((f32[32,1,48]{2,1,0:T(1,128)}), f32[32,1,48]{2,1,0:T(1,128)S(1)}, u32[]{:S(2)}, u32[]{:S(2)}) async-start(f32[32,1,48]{2,1,0:T(1,128)} %bitcast.19), calls=%async_computation.3 | async-start | bytes 32768 | tf_op jit(solution)/shard_map/all_to_all | solution.py:26
  173.6 0.7 compare_reduce_fusion
  174.3 6.2 %all-to-all-done.3 = f32[32,1,48]{2,1,0:T(1,128)S(1)} async-done(((f32[32,1,48]{2,1,0:T(1,128)}), f32[32,1,48]{2,1,0:T(1,128)S(1)}, u32[]{:S(2)}, u32[]{:S(2)}) %all-to-all-start.3) | async-done | bytes 6176 | tf_op jit(solution)/shard_map/all_to_all | solution.py:26
  180.5 0.1 reduce_sum.19
  180.5 0.6 broadcast_in_dim.6
  181.2 4.1 %all-to-all-start.4 = ((f32[32,1,48]{2,1,0:T(1,128)}), f32[32,1,48]{2,1,0:T(1,128)S(1)}, u32[]{:S(2)}, u32[]{:S(2)}) async-start(f32[32,1,48]{2,1,0:T(1,128)} %broadcast_in_dim.6), calls=%async_computation.4 | async-start | bytes 32768 | tf_op jit(solution)/shard_map/all_to_all | solution.py:29
  185.3 0.7 fusion.15
  186.0 3.7 %custom-call.12 = f32[1,48,48]{1,2,0:T(8,128)S(1)} custom-call(f32[1,48,48]{2,1,0:T(8,128)S(1)} %fusion.15), custom_call_target="InvertDiagBlocksLowerTriangular" | custom-call | tf_op jit(solution)/shard_map/jit(_cho_solve)/triangular_solve | solution.py:21
  189.7 2.6 all-to-all-done.4
  192.3 0.1 fusion.17
  192.5 0.2 convolution_bitcast_fusion
  192.6 9.9 %fusion.5 = f32[32,32,8,128]{3,1,0,2:T(8,128)S(1)} fusion(f32[32,32,8,128]{3,1,2,0:T(8,128)} %all-to-all-done, f32[48,32,1,1]{0,1,3,2:T(8,128)S(1)} %convolution_bitcast_fusion, f32[48,8,32,128]{3,1,2,0:T(8,128)} %bitcast.81, f32[32,8,128]{2,0,1:T(8,128)S(1)} %copy.21), kind=kOutput, calls=%fused_computation.6 | convolution fusion | flops 305135616 | bytes 14817280 | tf_op jit(solution)/shard_map/jk,krpc->pjrc/dot_general | solution.py:133
  202.6 0.5 copy.32
  203.1 55.3 %all_to_all.32 = f32[32,32,8,128]{3,1,2,0:T(8,128)S(1)} all-to-all(f32[32,32,8,128]{3,1,2,0:T(8,128)S(1)} %copy.32), channel_id=1, replica_groups=mesh['ang'=4,'pix'=32] {'pix'}, dimensions={0} | all-to-all | bytes 8388608 | tf_op jit(solution)/shard_map/all_to_all | solution.py:137
  258.4 4.4 %copy.49 = f32[32,32,8,128]{3,2,0,1:T(8,128)} copy(f32[32,32,8,128]{3,1,2,0:T(8,128)S(1)} %all_to_all.32) | data formatting | bytes 8388608 | tf_op jit(solution)/shard_map/all_to_all | solution.py:137
  (9 shorter events, 0.2 us)
Async XLA Ops:
  6.5 53.5 %copy-start = (f32[256,48]{0,1:T(8,128)S(1)}, f32[256,48]{0,1:T(8,128)}, u32[]{:S(2)}) copy-start(f32[256,48]{0,1:T(8,128)} %param.8) | copy-start | bytes 147460
  6.5 148.8 %all-gather.2.cloned.1.call-start = ((), (), s32[]{:S(2)}) async-start(), calls=%async_computation.6 | async-start | bytes 7864320 | tf_op jit(solution)/shard_map/all_gather | solution.py:121
  97.4 5.7 %copy-start.2 = (f32[8,1024]{1,0:T(8,128)S(1)}, f32[8,1024]{1,0:T(8,128)}, u32[]{:S(2)}) copy-start(f32[8,1024]{1,0:T(8,128)} %get-tuple-element.9.mean_ref) | copy-start | bytes 98308
  97.4 16.7 %copy-start.1 = (f32[48,256]{1,0:T(8,128)S(1)}, f32[48,256]{1,0:T(8,128)}, u32[]{:S(2)}) copy-start(f32[48,256]{1,0:T(8,128)} %fusion.9.lhs_ref) | copy-start | bytes 147460
  97.4 57.9 %all-to-all-start = ((f32[32,32,8,128]{3,1,2,0:T(8,128)}), f32[32,32,8,128]{3,1,2,0:T(8,128)}, u32[]{:S(2)}, u32[]{:S(2)}) async-start(f32[32,32,8,128]{3,1,2,0:T(8,128)} %copy.20), calls=%async_computation | async-start | bytes 8388608 | tf_op jit(solution)/shard_map/all_to_all | solution.py:104
  166.5 14.0 %all-to-all-start.3 = ((f32[32,1,48]{2,1,0:T(1,128)}), f32[32,1,48]{2,1,0:T(1,128)S(1)}, u32[]{:S(2)}, u32[]{:S(2)}) async-start(f32[32,1,48]{2,1,0:T(1,128)} %bitcast.19), calls=%async_computation.3 | async-start | bytes 32768 | tf_op jit(solution)/shard_map/all_to_all | solution.py:26
  181.2 11.1 %all-to-all-start.4 = ((f32[32,1,48]{2,1,0:T(1,128)}), f32[32,1,48]{2,1,0:T(1,128)S(1)}, u32[]{:S(2)}, u32[]{:S(2)}) async-start(f32[32,1,48]{2,1,0:T(1,128)} %broadcast_in_dim.6), calls=%async_computation.4 | async-start | bytes 32768 | tf_op jit(solution)/shard_map/all_to_all | solution.py:29
Sparse Core Ops, SparseCore 0:
  90.9 62.9 all-gather.1
where the time goes:
time: 270 us
  blocking collectives  104 us (39%)
  waiting for transfers between devices  45 us (17%)
  other arithmetic  29.2 us (11%)
  matrix products  24.1 us (9%)
  Pallas kernels  23.2 us (9%)
  starting transfers between devices  16.9 us (6%)
  local copies, waits for them, and re-layouts  13.8 us (5%)
  between operations  13.6 us (5%)
    all_to_all x1, blocking collectives, shards(): back = lax.all_to_all(tiles_out, 'pix', 0, 0, tiled=True)  55.3 us
    all_to_all x1, waiting for transfers between devices, shards(): tiles = lax.all_to_all(tiles_in, 'pix', 0, 0, tiled=True)  36.2 us
    all_to_all x1, blocking collectives, sum_by_exchange(): lax.all_to_all(rows.reshape(count, total // count, width), axes, 0, 0, ti...  22.2 us
    all_to_all x1, blocking collectives, sum_by_exchange(): gathered = lax.all_to_all(spread, axes, 0, 0, tiled=True)  15.2 us
    pallas_call x1, Pallas kernels, frame_gram(): pl.pallas_call(_gram_kernel, grid=(cols // width,), in_specs=[pl.BlockSpe...  13.7 us
    dot_general x1, matrix products, shards(): jnp.einsum('pjrc,krpc->jk', centred_frames, eigen_blk, precision=lax.Prec...  11.1 us
    all_gather x1, blocking collectives, shards(): mean_rows = lax.all_gather(mean_flat, 'ang', axis=1, tiled=True)  11 us
    another operation x6, other arithmetic, orthonormal(): lower = jnp.linalg.cholesky(correlation)  10.1 us
  transfers between devices with their start and end apart: 4, of which 3 were waited for; matrix products, arithmetic and copies ran while one was open for 6% of the time, Pallas kernels for 0%

commit v1 on v0

--- a/solution.py
+++ b/solution.py
@@ -122,18 +122,27 @@
         eigen_3d, "ang", axis=2, tiled=True
     )
     mean_rows = lax.all_gather(mean_flat, "ang", axis=1, tiled=True)
-    eigen_blk = eigen_rows.reshape(eigen_count, rows_dev, pix_count, cols_here)
-    mean_blk = mean_rows.reshape(rows_dev, pix_count, cols_here)
-    centred_frames = tiles - mean_blk.transpose(1, 0, 2)[:, None]
-    partial_value = jnp.einsum(
-        "pjrc,krpc->jk", centred_frames, eigen_blk, precision=lax.Precision.HIGH
+    group_blocks = cols_dev // cols_here
+    eigen_groups = eigen_rows.reshape(eigen_count, rows_dev, ang_count, group_blocks, cols_here)
+    mean_groups = mean_rows.reshape(rows_dev, ang_count, group_blocks, cols_here)
+    parts = []
+    for group in range(ang_count):
+        frames_g = tiles[group * group_blocks:(group + 1) * group_blocks]
+        mean_g = mean_groups[:, group].transpose(1, 0, 2)[:, None]
+        parts.append((eigen_groups[:, :, group], mean_g, frames_g))
+    partial_value = sum(
+        jnp.einsum("pjrc,krpc->jk", frames_g - mean_g, eigen_g, precision=lax.Precision.HIGH)
+        for eigen_g, mean_g, frames_g in parts
     )
     fit_rhs = sum_by_exchange(partial_value, "pix", pix_count) / npix
     weights = solve_normal(normal, fit_rhs)
-    estimate = mean_blk.transpose(1, 0, 2)[:, None] + jnp.einsum(
-        "jk,krpc->pjrc", weights, eigen_blk, precision=lax.Precision.HIGH
-    )
-    tiles_out = tiles / jnp.maximum(estimate, floor_value)
+    outs = []
+    for eigen_g, mean_g, frames_g in parts:
+        estimate = mean_g + jnp.einsum(
+            "jk,krpc->pjrc", weights, eigen_g, precision=lax.Precision.HIGH
+        )
+        outs.append(frames_g / jnp.maximum(estimate, floor_value))
+    tiles_out = jnp.concatenate(outs, axis=0)
     back = lax.all_to_all(tiles_out, "pix", 0, 0, tiled=True)
     result = back.transpose(1, 0, 2, 3).reshape(angle_count, rows_all, cols_here)
     return result

time: 270 us -> 283 us (1.048); the launches traced: 270 us -> 278 us
  local copies, waits for them, and re-layouts: 13.8 us -> 25.6 us
  matrix products: 24.1 us -> 19 us
    squeeze x0 -> x1, local copies, waits for them, and re-layouts: none -> 6.28 us  [shards(): parts.append((eigen_groups[:, :, group], mean_g, frames_g))]
    dot_general x2 -> x8, matrix products: 21.1 us -> 16 us  [the longest x4 8.21 us: shards(): jnp.einsum('pjrc,krpc->jk', frames_g - mean_g, eigen_g, precision=lax.Pre...]
    slice x0 -> x1, local copies, waits for them, and re-layouts: none -> 3.8 us  [shards(): frames_g = tiles[group * group_blocks:(group + 1) * group_blocks]]
  transfers between devices with their start and end apart: 4 -> 4, of which waited for: 3 -> 3; matrix products, arithmetic and copies ran while one was open for 6% -> 7% of each run, Pallas kernels for 0% -> 0%
where the time goes in v1:
time: 283 us; the launch traced here: 278 us
  blocking collectives  104 us (37%)
  waiting for transfers between devices  45.2 us (16%)
  other arithmetic  30 us (11%)
  local copies, waits for them, and re-layouts  25.6 us (9%)
  Pallas kernels  23.2 us (8%)
  matrix products  19 us (7%)
  starting transfers between devices  17.1 us (6%)
  between operations  14.2 us (5%)
    all_to_all x1, blocking collectives, shards(): back = lax.all_to_all(tiles_out, 'pix', 0, 0, tiled=True)  55.2 us
    all_to_all x1, waiting for transfers between devices, shards(): tiles = lax.all_to_all(tiles_in, 'pix', 0, 0, tiled=True)  36.2 us
    all_to_all x1, blocking collectives, sum_by_exchange(): lax.all_to_all(rows.reshape(count, total // count, width), axes, 0, 0, ti...  22.2 us
    all_to_all x1, blocking collectives, sum_by_exchange(): gathered = lax.all_to_all(spread, axes, 0, 0, tiled=True)  15.6 us
    pallas_call x1, Pallas kernels, frame_gram(): pl.pallas_call(_gram_kernel, grid=(cols // width,), in_specs=[pl.BlockSpe...  13.7 us
    all_gather x1, blocking collectives, shards(): mean_rows = lax.all_gather(mean_flat, 'ang', axis=1, tiled=True)  11 us
    another operation x6, other arithmetic, orthonormal(): lower = jnp.linalg.cholesky(correlation)  10.1 us
    pallas_call x1, Pallas kernels, project_rows(): pl.pallas_call(_project_kernel, grid=(1,), in_specs=[pl.BlockSpec((m, k),...  9.5 us
  transfers between devices with their start and end apart: 4, of which 3 were waited for; matrix products, arithmetic and copies ran while one was open for 7% of the time, Pallas kernels for 0%

profile of v1, /device:TPU:1, one launch (start us, length us, event | category | flops | bytes accessed | tf_op | source)
XLA Modules:
  0.0 278.3 jit_solution(10978233756867063941)
XLA Ops:
  6.5 13.7 %shard_map.37 = (f32[256,256]{1,0:T(8,128)}, f32[8,1024]{1,0:T(8,128)}) custom-call(f32[256,8,1024]{2,1,0:T(8,128)} %flats_ref.3), custom_call_target="tpu_custom_call" | custom-call | tf_op jit(solution)/shard_map/pallas_call | solution.py:55
  20.2 1.2 reshape_reshape.5
  21.5 22.2 %all_to_all.30 = f32[128,1,512]{2,1,0:T(1,128)S(1)} all-to-all(f32[128,1,512]{2,1,0:T(1,128)S(1)} %reshape_reshape.5), channel_id=1, replica_groups=mesh['ang'=4,'pix'=32] {'ang','pix'}, dimensions={0} | all-to-all | bytes 524288 | tf_op jit(solution)/shard_map/all_to_all | solution.py:26
  43.7 0.2 reduce_sum.18
  43.9 0.1 broadcast_in_dim.4
  44.0 15.6 %all_to_all.31 = f32[128,1,512]{2,1,0:T(1,128)S(1)} all-to-all(f32[128,1,512]{2,1,0:T(1,128)S(1)} %broadcast_in_dim.4), channel_id=1, replica_groups=mesh['ang'=4,'pix'=32] {'ang','pix'}, dimensions={0} | all-to-all | bytes 524288 | tf_op jit(solution)/shard_map/all_to_all | solution.py:29
  59.6 0.7 multiply_reduce_fusion
  60.4 0.4 fusion.89
  60.8 0.2 fusion.90
  60.9 0.1 copy.48
  61.0 4.4 %cholesky.59 = f32[48,48]{1,0:T(8,128)S(1)} custom-call(f32[48,48]{1,0:T(8,128)S(1)} %fusion.85), custom_call_target="Cholesky" | custom-call | tf_op jit(solution)/shard_map/jit(cholesky)/cholesky | solution.py:15
  65.5 0.6 compare_reduce_fusion.2
  66.1 0.7 fusion.75
  66.8 3.7 %custom-call.14 = f32[1,48,48]{1,2,0:T(8,128)S(1)} custom-call(f32[1,48,48]{2,1,0:T(8,128)S(1)} %fusion.75), custom_call_target="InvertDiagBlocksLowerTriangular" | custom-call | tf_op jit(solution)/shard_map/jit(_solve_triangular)/triangular_solve | solution.py:16
  70.4 0.3 fusion.73
  70.7 0.4 fusion.91
  71.0 0.2 fusion.92
  71.2 0.1 copy.49
  71.3 4.4 %cholesky.70 = f32[48,48]{1,0:T(8,128)S(1)} custom-call(f32[48,48]{1,0:T(8,128)S(1)} %fusion.83), custom_call_target="Cholesky" | custom-call | tf_op jit(solution)/shard_map/jit(cholesky)/cholesky | solution.py:15
  75.7 0.6 compare_reduce_fusion.1
  76.4 0.7 fusion.76
  77.0 3.7 %custom-call.15 = f32[1,48,48]{1,2,0:T(8,128)S(1)} custom-call(f32[1,48,48]{2,1,0:T(8,128)S(1)} %fusion.76), custom_call_target="InvertDiagBlocksLowerTriangular" | custom-call | tf_op jit(solution)/shard_map/jit(_solve_triangular)/triangular_solve | solution.py:16
  80.7 0.9 fusion.71.lhs_ref
  81.6 9.5 %shard_map.38 = f32[48,8,1024]{2,1,0:T(8,128)} custom-call(f32[48,256]{1,0:T(8,128)} %fusion.71.lhs_ref, f32[256,8,1024]{2,1,0:T(8,128)} %flats_ref.3, f32[8,1024]{1,0:T(8,128)} %get-tuple-element.9.mean_ref), custom_call_target="tpu_custom_call" | custom-call | tf_op jit(solution)/shard_map/pallas_call | solution.py:83
  91.1 0.0 all-gather.2.cloned.1.call-update
  91.1 6.6 %copy.44 = f32[32,32,8,128]{3,1,2,0:T(8,128)} copy(f32[32,32,8,128]{3,2,0,1:T(8,128)} %bitcast.176) | data formatting | bytes 8388608 | tf_op jit(solution)/shard_map/transpose | solution.py:103
  97.7 5.6 %all-to-all-start = ((f32[32,32,8,128]{3,1,2,0:T(8,128)}), f32[32,32,8,128]{3,1,2,0:T(8,128)}, u32[]{:S(2)}, u32[]{:S(2)}) async-start(f32[32,32,8,128]{3,1,2,0:T(8,128)} %copy.44), calls=%async_computation | async-start | bytes 8388608 | tf_op jit(solution)/shard_map/all_to_all | solution.py:104
  103.3 11.0 %all_gather.6 = f32[8,4096]{1,0:T(8,128)S(1)} all-gather(f32[8,1024]{1,0:T(8,128)S(1)} %copy-done.11), channel_id=1, replica_groups=mesh['ang'=4,'pix'=32] {'ang'}, dimensions={1}, use_global_device_ids=true | all-gather | bytes 163840 | tf_op jit(solution)/shard_map/all_gather | solution.py:124
  114.4 0.4 fusion.93
  114.8 0.2 fusion.94
  114.9 0.1 copy.51
  115.0 4.4 %cholesky.81 = f32[48,48]{1,0:T(8,128)S(1)} custom-call(f32[48,48]{1,0:T(8,128)S(1)} %fusion.81), custom_call_target="Cholesky" | custom-call | tf_op jit(solution)/shard_map/jit(cholesky)/cholesky | solution.py:20
  119.5 36.2 %all-to-all-done = f32[32,32,8,128]{3,1,2,0:T(8,128)} async-done(((f32[32,32,8,128]{3,1,2,0:T(8,128)}), f32[32,32,8,128]{3,1,2,0:T(8,128)}, u32[]{:S(2)}, u32[]{:S(2)}) %all-to-all-start) | async-done | bytes 4194336 | tf_op jit(solution)/shard_map/all_to_all | solution.py:104
  155.6 3.8 %fusion.88 = (f32[8,32,8,128]{3,1,2,0:T(8,128)}, f32[8,32,8,128]{3,1,2,0:T(8,128)S(1)}, f32[8,32,8,128]{3,1,2,0:T(8,128)S(1)}, f32[8,32,8,128]{3,1,2,0:T(8,128)S(1)}) fusion(f32[32,32,8,128]{3,1,2,0:T(8,128)} %all-to-all-done), kind=kLoop, calls=%fused_computation.90 | loop fusion | bytes 8388608 | tf_op jit(solution)/shard_map/slice | solution.py:130
  159.4 1.0 copy-done.2
  160.4 0.4 copy-done.4
  160.8 0.4 copy_subtract_fusion.1
  161.2 0.0 all-gather.2.cloned.1.call-done
  161.2 6.3 %slice_bitcast_fusion.7 = (f32[48,8,8,128]{3,1,2,0:T(8,128)}, f32[48,8,8,128]{3,1,2,0:T(8,128)}, f32[48,8,8,128]{3,1,2,0:T(8,128)}, f32[48,8,8,128]{3,1,2,0:T(8,...) fusion(f32[48,8,4,8,128]{4,1,3,2,0:T(8,128)} %bitcast.175), kind=kLoop, calls=%fused_computation.89 | loop fusion | bytes 18874368 | tf_op jit(solution)/shard_map/squeeze | solution.py:132
  167.5 1.9 fusion.60
  169.4 1.9 fusion.66
  171.3 1.9 fusion.65
  173.2 0.0 copy-done.6
  173.2 2.5 fusion.64
  175.8 7.1 %all-to-all-start.3 = ((f32[32,1,48]{2,1,0:T(1,128)}), f32[32,1,48]{2,1,0:T(1,128)S(1)}, u32[]{:S(2)}, u32[]{:S(2)}) async-start(f32[32,1,48]{2,1,0:T(1,128)} %bitcast.36), calls=%async_computation.3 | async-start | bytes 32768 | tf_op jit(solution)/shard_map/all_to_all | solution.py:26
  182.9 0.6 compare_reduce_fusion
  183.6 6.3 %all-to-all-done.3 = f32[32,1,48]{2,1,0:T(1,128)S(1)} async-done(((f32[32,1,48]{2,1,0:T(1,128)}), f32[32,1,48]{2,1,0:T(1,128)S(1)}, u32[]{:S(2)}, u32[]{:S(2)}) %all-to-all-start.3) | async-done | bytes 6176 | tf_op jit(solution)/shard_map/all_to_all | solution.py:26
  189.9 0.1 reduce_sum.19
  189.9 0.6 broadcast_in_dim.6
  190.5 4.4 %all-to-all-start.4 = ((f32[32,1,48]{2,1,0:T(1,128)}), f32[32,1,48]{2,1,0:T(1,128)S(1)}, u32[]{:S(2)}, u32[]{:S(2)}) async-start(f32[32,1,48]{2,1,0:T(1,128)} %broadcast_in_dim.6), calls=%async_computation.4 | async-start | bytes 32768 | tf_op jit(solution)/shard_map/all_to_all | solution.py:29
  194.9 0.6 fusion.77
  195.6 3.7 %custom-call.12 = f32[1,48,48]{1,2,0:T(8,128)S(1)} custom-call(f32[1,48,48]{2,1,0:T(8,128)S(1)} %fusion.77), custom_call_target="InvertDiagBlocksLowerTriangular" | custom-call | tf_op jit(solution)/shard_map/jit(_cho_solve)/triangular_solve | solution.py:21
  199.2 2.7 all-to-all-done.4
  202.0 0.1 fusion.79
  202.2 0.2 convolution_bitcast_fusion
  202.3 3.0 %fusion.39 = f32[8,32,8,128]{3,1,0,2:T(8,128)S(1)} fusion(f32[48,32,1,1]{0,1,3,2:T(8,128)S(1)} %convolution_bitcast_fusion, f32[48,8,8,128]{3,1,2,0:T(8,128)} %get-tuple-element.14, f32[8,32,8,128]{3,1,2,0:T(8,128)S(1)} %copy-done.6, f32[8,8,128]{2,0,1:T(8,128)S(1)} %copy.62), kind=kOutput, calls=%fused_computation.27 | convolution fusion | flops 76283904 | bytes 3708928 | tf_op jit(solution)/shard_map/jk,krpc->pjrc/dot_general | solution.py:141
  205.4 1.6 fusion.45
  207.0 0.1 copy-done.8
  207.2 1.6 fusion.51
  208.7 1.6 fusion.57
  210.3 0.4 pad_maximum_fusion
  210.8 0.6 copy.70
  211.4 55.2 %all_to_all.32 = f32[32,32,8,128]{3,1,2,0:T(8,128)S(1)} all-to-all(f32[32,32,8,128]{3,1,2,0:T(8,128)S(1)} %copy.70), channel_id=1, replica_groups=mesh['ang'=4,'pix'=32] {'pix'}, dimensions={0} | all-to-all | bytes 8388608 | tf_op jit(solution)/shard_map/all_to_all | solution.py:146
  266.6 4.4 %copy.172 = f32[32,32,8,128]{3,2,0,1:T(8,128)} copy(f32[32,32,8,128]{3,1,2,0:T(8,128)S(1)} %all_to_all.32) | data formatting | bytes 8388608 | tf_op jit(solution)/shard_map/all_to_all | solution.py:146
  (34 shorter events, 0.3 us)
Async XLA Ops:
  6.5 53.8 %copy-start = (f32[256,48]{0,1:T(8,128)S(1)}, f32[256,48]{0,1:T(8,128)}, u32[]{:S(2)}) copy-start(f32[256,48]{0,1:T(8,128)} %param.8) | copy-start | bytes 147460
  6.5 154.7 %all-gather.2.cloned.1.call-start = ((), (), s32[]{:S(2)}) async-start(), calls=%async_computation.6 | async-start | bytes 7864320 | tf_op jit(solution)/shard_map/all_gather | solution.py:121
  97.7 5.6 %copy-start.11 = (f32[8,1024]{1,0:T(8,128)S(1)}, f32[8,1024]{1,0:T(8,128)}, u32[]{:S(2)}) copy-start(f32[8,1024]{1,0:T(8,128)} %get-tuple-element.9.mean_ref) | copy-start | bytes 98308
  97.7 16.6 %copy-start.10 = (f32[48,256]{1,0:T(8,128)S(1)}, f32[48,256]{1,0:T(8,128)}, u32[]{:S(2)}) copy-start(f32[48,256]{1,0:T(8,128)} %fusion.71.lhs_ref) | copy-start | bytes 147460
  97.7 57.9 %all-to-all-start = ((f32[32,32,8,128]{3,1,2,0:T(8,128)}), f32[32,32,8,128]{3,1,2,0:T(8,128)}, u32[]{:S(2)}, u32[]{:S(2)}) async-start(f32[32,32,8,128]{3,1,2,0:T(8,128)} %copy.44), calls=%async_computation | async-start | bytes 8388608 | tf_op jit(solution)/shard_map/all_to_all | solution.py:104
  159.4 1.0 copy-start.2
  159.4 1.4 copy-start.4
  171.3 1.9 copy-start.6
  175.8 14.1 %all-to-all-start.3 = ((f32[32,1,48]{2,1,0:T(1,128)}), f32[32,1,48]{2,1,0:T(1,128)S(1)}, u32[]{:S(2)}, u32[]{:S(2)}) async-start(f32[32,1,48]{2,1,0:T(1,128)} %bitcast.36), calls=%async_computation.3 | async-start | bytes 32768 | tf_op jit(solution)/shard_map/all_to_all | solution.py:26
  190.5 11.5 %all-to-all-start.4 = ((f32[32,1,48]{2,1,0:T(1,128)}), f32[32,1,48]{2,1,0:T(1,128)S(1)}, u32[]{:S(2)}, u32[]{:S(2)}) async-start(f32[32,1,48]{2,1,0:T(1,128)} %broadcast_in_dim.6), calls=%async_computation.4 | async-start | bytes 32768 | tf_op jit(solution)/shard_map/all_to_all | solution.py:29
  202.3 3.1 %copy-start.5 = (f32[8,32,8,128]{3,1,2,0:T(8,128)S(1)}, f32[8,32,8,128]{3,1,2,0:T(8,128)}, u32[]{:S(2)}) copy-start(f32[8,32,8,128]{3,1,2,0:T(8,128)} %copy-done.4) | copy-start | bytes 3145732
  202.3 3.1 %copy-start.9 = (f32[48,8,8,128]{3,1,2,0:T(8,128)S(1)}, f32[48,8,8,128]{3,1,2,0:T(8,128)}, u32[]{:S(2)}) copy-start(f32[48,8,8,128]{3,1,2,0:T(8,128)} %get-tuple-element.13) | copy-start | bytes 4718596
  205.4 1.6 copy-start.3
  205.4 1.7 copy-start.8
  207.2 1.6 copy-start.7
  266.6 4.4 %copy-start.1 = (f32[256,48]{0,1:T(8,128)S(1)}, f32[256,48]{0,1:T(8,128)}, u32[]{:S(2)}) copy-start(f32[256,48]{0,1:T(8,128)} %param.8) | copy-start | bytes 147460
Sparse Core Ops, SparseCore 0:
  91.2 62.7 all-gather.1

commit v2 on v0

--- a/solution.py
+++ b/solution.py
@@ -71,7 +71,7 @@
     lhs = lhs_ref[...]
     for row in range(flats_ref.shape[1]):
         centred = flats_ref[:, row, :] - mean_ref[row, :][None, :]
-        out_ref[:, row, :] = jnp.dot(
+        out_ref[row] = jnp.dot(
             lhs, centred, precision=lax.Precision.HIGH,
             preferred_element_type=jnp.float32,
         )
@@ -88,8 +88,8 @@
             pl.BlockSpec((k, rows, width), lambda r: (0, 0, 0)),
             pl.BlockSpec((rows, width), lambda r: (0, 0)),
         ],
-        out_specs=pl.BlockSpec((m, rows, width), lambda r: (0, 0, 0)),
-        out_shape=jax.ShapeDtypeStruct((m, rows, width), jnp.float32),
+        out_specs=pl.BlockSpec((rows, m, width), lambda r: (0, 0, 0)),
+        out_shape=jax.ShapeDtypeStruct((rows, m, width), jnp.float32),
     )(lhs, flats, mean)
 
 
@@ -111,27 +111,26 @@
     for turn in range(SUBSPACE):
         basis = orthonormal(jnp.dot(gram, basis, precision=lax.Precision.HIGHEST))
     eigen_3d = project_rows(basis.T, flats, mean_flat)
-    eigen_flats = eigen_3d.reshape(basis.shape[1], -1)
     normal = jnp.dot(
         basis.T,
         jnp.dot(gram, basis, precision=lax.Precision.HIGHEST),
         precision=lax.Precision.HIGHEST,
     )
-    eigen_count = eigen_flats.shape[0]
+    eigen_count = basis.shape[1]
     eigen_rows = lax.all_gather(
         eigen_3d, "ang", axis=2, tiled=True
     )
     mean_rows = lax.all_gather(mean_flat, "ang", axis=1, tiled=True)
-    eigen_blk = eigen_rows.reshape(eigen_count, rows_dev, pix_count, cols_here)
+    eigen_blk = eigen_rows.reshape(rows_dev, eigen_count, pix_count, cols_here)
     mean_blk = mean_rows.reshape(rows_dev, pix_count, cols_here)
     centred_frames = tiles - mean_blk.transpose(1, 0, 2)[:, None]
     partial_value = jnp.einsum(
-        "pjrc,krpc->jk", centred_frames, eigen_blk, precision=lax.Precision.HIGH
+        "pjrc,rkpc->jk", centred_frames, eigen_blk, precision=lax.Precision.HIGH
     )
     fit_rhs = sum_by_exchange(partial_value, "pix", pix_count) / npix
     weights = solve_normal(normal, fit_rhs)
     estimate = mean_blk.transpose(1, 0, 2)[:, None] + jnp.einsum(
-        "jk,krpc->pjrc", weights, eigen_blk, precision=lax.Precision.HIGH
+        "jk,rkpc->pjrc", weights, eigen_blk, precision=lax.Precision.HIGH
     )
     tiles_out = tiles / jnp.maximum(estimate, floor_value)
     back = lax.all_to_all(tiles_out, "pix", 0, 0, tiled=True)

time: 270 us -> 263 us (0.974)
  matrix products: 24.1 us -> 17.1 us
    dot_general x2, matrix products: 21.1 us -> 14.1 us  [the longest x1 7.47 us: shards(): jnp.einsum('pjrc,rkpc->jk', centred_frames, eigen_blk, precision=lax.Prec...]
where the time goes in v2:
time: 263 us; the launch traced here: 262 us
  blocking collectives  104 us (40%)
  waiting for transfers between devices  45 us (17%)
  other arithmetic  29.2 us (11%)
  Pallas kernels  22.7 us (9%)
  matrix products  17.1 us (7%)
  starting transfers between devices  16.9 us (6%)
  local copies, waits for them, and re-layouts  13.8 us (5%)
  between operations  13.6 us (5%)
    all_to_all x1, blocking collectives, shards(): back = lax.all_to_all(tiles_out, 'pix', 0, 0, tiled=True)  55.3 us
    all_to_all x1, waiting for transfers between devices, shards(): tiles = lax.all_to_all(tiles_in, 'pix', 0, 0, tiled=True)  36.2 us
    all_to_all x1, blocking collectives, sum_by_exchange(): lax.all_to_all(rows.reshape(count, total // count, width), axes, 0, 0, ti...  22.2 us
    all_to_all x1, blocking collectives, sum_by_exchange(): gathered = lax.all_to_all(spread, axes, 0, 0, tiled=True)  15.2 us
    pallas_call x1, Pallas kernels, frame_gram(): pl.pallas_call(_gram_kernel, grid=(cols // width,), in_specs=[pl.BlockSpe...  13.7 us
    all_gather x1, blocking collectives, shards(): mean_rows = lax.all_gather(mean_flat, 'ang', axis=1, tiled=True)  11 us
    another operation x6, other arithmetic, orthonormal(): lower = jnp.linalg.cholesky(correlation)  10.1 us
    pallas_call x1, Pallas kernels, project_rows(): pl.pallas_call(_project_kernel, grid=(1,), in_specs=[pl.BlockSpec((m, k),...  8.96 us
  transfers between devices with their start and end apart: 4, of which 3 were waited for; matrix products, arithmetic and copies ran while one was open for 6% of the time, Pallas kernels for 0%

profile of v2, /device:TPU:1, one launch (start us, length us, event | category | flops | bytes accessed | tf_op | source)
XLA Modules:
  0.0 262.1 jit_solution(14719715735388681034)
XLA Ops:
  6.5 0.0 copy-start
  6.5 0.0 all-gather.2.cloned.1.call-start
  6.5 13.7 %shard_map.37 = (f32[256,256]{1,0:T(8,128)}, f32[8,1024]{1,0:T(8,128)}) custom-call(f32[256,8,1024]{2,1,0:T(8,128)} %flats_ref.3), custom_call_target="tpu_custom_call" | custom-call | tf_op jit(solution)/shard_map/pallas_call | solution.py:55
  20.2 1.2 reshape_reshape.5
  21.5 22.2 %all_to_all.30 = f32[128,1,512]{2,1,0:T(1,128)S(1)} all-to-all(f32[128,1,512]{2,1,0:T(1,128)S(1)} %reshape_reshape.5), channel_id=1, replica_groups=mesh['ang'=4,'pix'=32] {'ang','pix'}, dimensions={0} | all-to-all | bytes 524288 | tf_op jit(solution)/shard_map/all_to_all | solution.py:26
  43.7 0.2 reduce_sum.18
  43.9 0.1 broadcast_in_dim.4
  44.1 15.2 %all_to_all.31 = f32[128,1,512]{2,1,0:T(1,128)S(1)} all-to-all(f32[128,1,512]{2,1,0:T(1,128)S(1)} %broadcast_in_dim.4), channel_id=1, replica_groups=mesh['ang'=4,'pix'=32] {'ang','pix'}, dimensions={0} | all-to-all | bytes 524288 | tf_op jit(solution)/shard_map/all_to_all | solution.py:29
  59.3 0.7 multiply_reduce_fusion
  60.0 0.0 copy-done
  60.1 0.4 fusion.28
  60.4 0.2 fusion.29
  60.6 0.1 copy.23
  60.7 4.4 %cholesky.59 = f32[48,48]{1,0:T(8,128)S(1)} custom-call(f32[48,48]{1,0:T(8,128)S(1)} %fusion.25), custom_call_target="Cholesky" | custom-call | tf_op jit(solution)/shard_map/jit(cholesky)/cholesky | solution.py:15
  65.1 0.6 compare_reduce_fusion.2
  65.8 0.7 fusion.15
  66.4 3.7 %custom-call.14 = f32[1,48,48]{1,2,0:T(8,128)S(1)} custom-call(f32[1,48,48]{2,1,0:T(8,128)S(1)} %fusion.15), custom_call_target="InvertDiagBlocksLowerTriangular" | custom-call | tf_op jit(solution)/shard_map/jit(_solve_triangular)/triangular_solve | solution.py:16
  70.1 0.2 fusion.13
  70.3 0.4 fusion.30
  70.7 0.2 fusion.31
  70.9 0.1 copy.24
  71.0 4.4 %cholesky.70 = f32[48,48]{1,0:T(8,128)S(1)} custom-call(f32[48,48]{1,0:T(8,128)S(1)} %fusion.23), custom_call_target="Cholesky" | custom-call | tf_op jit(solution)/shard_map/jit(cholesky)/cholesky | solution.py:15
  75.4 0.6 compare_reduce_fusion.1
  76.0 0.7 fusion.16
  76.7 3.7 %custom-call.15 = f32[1,48,48]{1,2,0:T(8,128)S(1)} custom-call(f32[1,48,48]{2,1,0:T(8,128)S(1)} %fusion.16), custom_call_target="InvertDiagBlocksLowerTriangular" | custom-call | tf_op jit(solution)/shard_map/jit(_solve_triangular)/triangular_solve | solution.py:16
  80.4 0.9 fusion.11.lhs_ref
  81.3 9.0 %shard_map.38 = f32[8,48,1024]{2,1,0:T(8,128)} custom-call(f32[48,256]{1,0:T(8,128)} %fusion.11.lhs_ref, f32[256,8,1024]{2,1,0:T(8,128)} %flats_ref.3, f32[8,1024]{1,0:T(8,128)} %get-tuple-element.9.mean_ref), custom_call_target="tpu_custom_call" | custom-call | tf_op jit(solution)/shard_map/pallas_call | solution.py:83
  90.2 0.0 all-gather.2.cloned.1.call-update
  90.2 6.6 %copy.20 = f32[32,32,8,128]{3,1,2,0:T(8,128)} copy(f32[32,32,8,128]{3,2,0,1:T(8,128)} %bitcast.95) | data formatting | bytes 8388608 | tf_op jit(solution)/shard_map/transpose | solution.py:103
  96.9 0.0 copy-start.2
  96.9 0.0 copy-start.1
  96.9 5.7 %all-to-all-start = ((f32[32,32,8,128]{3,1,2,0:T(8,128)}), f32[32,32,8,128]{3,1,2,0:T(8,128)}, u32[]{:S(2)}, u32[]{:S(2)}) async-start(f32[32,32,8,128]{3,1,2,0:T(8,128)} %copy.20), calls=%async_computation | async-start | bytes 8388608 | tf_op jit(solution)/shard_map/all_to_all | solution.py:104
  102.5 0.0 copy-done.2
  102.5 11.0 %all_gather.6 = f32[8,4096]{1,0:T(8,128)S(1)} all-gather(f32[8,1024]{1,0:T(8,128)S(1)} %copy-done.2), channel_id=1, replica_groups=mesh['ang'=4,'pix'=32] {'ang'}, dimensions={1}, use_global_device_ids=true | all-gather | bytes 163840 | tf_op jit(solution)/shard_map/all_gather | solution.py:123
  113.5 0.0 copy-done.1
  113.6 0.4 fusion.32
  113.9 0.2 fusion.33
  114.1 0.1 copy.25
  114.2 4.4 %cholesky.81 = f32[48,48]{1,0:T(8,128)S(1)} custom-call(f32[48,48]{1,0:T(8,128)S(1)} %fusion.21), custom_call_target="Cholesky" | custom-call | tf_op jit(solution)/shard_map/jit(cholesky)/cholesky | solution.py:20
  118.6 36.2 %all-to-all-done = f32[32,32,8,128]{3,1,2,0:T(8,128)} async-done(((f32[32,32,8,128]{3,1,2,0:T(8,128)}), f32[32,32,8,128]{3,1,2,0:T(8,128)}, u32[]{:S(2)}, u32[]{:S(2)}) %all-to-all-start) | async-done | bytes 4194336 | tf_op jit(solution)/shard_map/all_to_all | solution.py:104
  154.8 0.0 all-gather.2.cloned.1.call-done
  154.8 7.5 %fusion = f32[32,48,1,1]{1,0,3,2:T(8,128)} fusion(f32[8,48,4096]{2,1,0:T(8,128)} %all-gather.2.cloned.1.call-done, f32[32,32,8,128]{3,1,2,0:T(8,128)} %all-to-all-done, f32[32,8,128]{2,0,1:T(8,128)S(1)} %copy.21), kind=kOutput, calls=%fused_computation | convolution fusion | flops 303038464 | bytes 10622976 | tf_op jit(solution)/shard_map/pjrc,rkpc->jk/dot_general | solution.py:127
  162.3 7.1 %all-to-all-start.3 = ((f32[32,1,48]{2,1,0:T(1,128)}), f32[32,1,48]{2,1,0:T(1,128)S(1)}, u32[]{:S(2)}, u32[]{:S(2)}) async-start(f32[32,1,48]{2,1,0:T(1,128)} %bitcast.18), calls=%async_computation.3 | async-start | bytes 32768 | tf_op jit(solution)/shard_map/all_to_all | solution.py:26
  169.4 0.7 compare_reduce_fusion
  170.1 6.2 %all-to-all-done.3 = f32[32,1,48]{2,1,0:T(1,128)S(1)} async-done(((f32[32,1,48]{2,1,0:T(1,128)}), f32[32,1,48]{2,1,0:T(1,128)S(1)}, u32[]{:S(2)}, u32[]{:S(2)}) %all-to-all-start.3) | async-done | bytes 6176 | tf_op jit(solution)/shard_map/all_to_all | solution.py:26
  176.3 0.1 reduce_sum.19
  176.3 0.6 broadcast_in_dim.6
  177.0 4.1 %all-to-all-start.4 = ((f32[32,1,48]{2,1,0:T(1,128)}), f32[32,1,48]{2,1,0:T(1,128)S(1)}, u32[]{:S(2)}, u32[]{:S(2)}) async-start(f32[32,1,48]{2,1,0:T(1,128)} %broadcast_in_dim.6), calls=%async_computation.4 | async-start | bytes 32768 | tf_op jit(solution)/shard_map/all_to_all | solution.py:29
  181.1 0.7 fusion.17
  181.8 3.7 %custom-call.12 = f32[1,48,48]{1,2,0:T(8,128)S(1)} custom-call(f32[1,48,48]{2,1,0:T(8,128)S(1)} %fusion.17), custom_call_target="InvertDiagBlocksLowerTriangular" | custom-call | tf_op jit(solution)/shard_map/jit(_cho_solve)/triangular_solve | solution.py:21
  185.5 2.6 %all-to-all-done.4 = f32[32,1,48]{2,1,0:T(1,128)S(1)} async-done(((f32[32,1,48]{2,1,0:T(1,128)}), f32[32,1,48]{2,1,0:T(1,128)S(1)}, u32[]{:S(2)}, u32[]{:S(2)}) %all-to-all-start.4) | async-done | bytes 6176 | tf_op jit(solution)/shard_map/all_to_all | solution.py:29
  188.1 0.1 fusion.19
  188.3 0.2 convolution_bitcast_fusion
  188.4 6.6 %fusion.7 = f32[32,32,8,128]{3,1,0,2:T(8,128)S(1)} fusion(f32[32,32,8,128]{3,1,2,0:T(8,128)} %all-to-all-done, f32[48,32,1,1]{0,1,3,2:T(8,128)S(1)} %convolution_bitcast_fusion, f32[32,8,128]{2,0,1:T(8,128)S(1)} %copy.21, f32[8,48,4096]{2,1,0:T(8,128)} %all-gather.2.cloned.1.call-done), kind=kOutput, calls=%fused_computation.8 | convolution fusion | flops 305135616 | bytes 14817280 | tf_op jit(solution)/shard_map/jk,rkpc->pjrc/dot_general | solution.py:132
  195.0 0.5 copy.32
  195.5 55.3 %all_to_all.32 = f32[32,32,8,128]{3,1,2,0:T(8,128)S(1)} all-to-all(f32[32,32,8,128]{3,1,2,0:T(8,128)S(1)} %copy.32), channel_id=1, replica_groups=mesh['ang'=4,'pix'=32] {'pix'}, dimensions={0} | all-to-all | bytes 8388608 | tf_op jit(solution)/shard_map/all_to_all | solution.py:136
  250.8 4.4 %copy.55 = f32[32,32,8,128]{3,2,0,1:T(8,128)} copy(f32[32,32,8,128]{3,1,2,0:T(8,128)S(1)} %all_to_all.32) | data formatting | bytes 8388608 | tf_op jit(solution)/shard_map/all_to_all | solution.py:136
  (9 shorter events, 0.2 us)
Async XLA Ops:
  6.5 53.5 %copy-start = (f32[256,48]{0,1:T(8,128)S(1)}, f32[256,48]{0,1:T(8,128)}, u32[]{:S(2)}) copy-start(f32[256,48]{0,1:T(8,128)} %param.8) | copy-start | bytes 147460
  6.5 148.3 %all-gather.2.cloned.1.call-start = ((), (), s32[]{:S(2)}) async-start(), calls=%async_computation.6 | async-start | bytes 7864320 | tf_op jit(solution)/shard_map/all_gather | solution.py:120
  96.9 5.7 %copy-start.2 = (f32[8,1024]{1,0:T(8,128)S(1)}, f32[8,1024]{1,0:T(8,128)}, u32[]{:S(2)}) copy-start(f32[8,1024]{1,0:T(8,128)} %get-tuple-element.9.mean_ref) | copy-start | bytes 98308
  96.9 16.7 %copy-start.1 = (f32[48,256]{1,0:T(8,128)S(1)}, f32[48,256]{1,0:T(8,128)}, u32[]{:S(2)}) copy-start(f32[48,256]{1,0:T(8,128)} %fusion.11.lhs_ref) | copy-start | bytes 147460
  96.9 57.9 %all-to-all-start = ((f32[32,32,8,128]{3,1,2,0:T(8,128)}), f32[32,32,8,128]{3,1,2,0:T(8,128)}, u32[]{:S(2)}, u32[]{:S(2)}) async-start(f32[32,32,8,128]{3,1,2,0:T(8,128)} %copy.20), calls=%async_computation | async-start | bytes 8388608 | tf_op jit(solution)/shard_map/all_to_all | solution.py:104
  162.3 14.0 %all-to-all-start.3 = ((f32[32,1,48]{2,1,0:T(1,128)}), f32[32,1,48]{2,1,0:T(1,128)S(1)}, u32[]{:S(2)}, u32[]{:S(2)}) async-start(f32[32,1,48]{2,1,0:T(1,128)} %bitcast.18), calls=%async_computation.3 | async-start | bytes 32768 | tf_op jit(solution)/shard_map/all_to_all | solution.py:26
  177.0 11.1 %all-to-all-start.4 = ((f32[32,1,48]{2,1,0:T(1,128)}), f32[32,1,48]{2,1,0:T(1,128)S(1)}, u32[]{:S(2)}, u32[]{:S(2)}) async-start(f32[32,1,48]{2,1,0:T(1,128)} %broadcast_in_dim.6), calls=%async_computation.4 | async-start | bytes 32768 | tf_op jit(solution)/shard_map/all_to_all | solution.py:29
Sparse Core Ops, SparseCore 0:
  90.4 62.9 all-gather.1

commit v3 on v2

--- a/solution.py
+++ b/solution.py
@@ -77,18 +77,18 @@
         )
 
 
-def project_rows(lhs, flats, mean):
+def project_rows(lhs, flats, mean, block=256):
     m, k = lhs.shape
     _, rows, width = flats.shape
     return pl.pallas_call(
         _project_kernel,
-        grid=(1,),
+        grid=(width // block,),
         in_specs=[
-            pl.BlockSpec((m, k), lambda r: (0, 0)),
-            pl.BlockSpec((k, rows, width), lambda r: (0, 0, 0)),
-            pl.BlockSpec((rows, width), lambda r: (0, 0)),
+            pl.BlockSpec((m, k), lambda i: (0, 0)),
+            pl.BlockSpec((k, rows, block), lambda i: (0, 0, i)),
+            pl.BlockSpec((rows, block), lambda i: (0, i)),
         ],
-        out_specs=pl.BlockSpec((rows, m, width), lambda r: (0, 0, 0)),
+        out_specs=pl.BlockSpec((rows, m, block), lambda i: (0, 0, i)),
         out_shape=jax.ShapeDtypeStruct((rows, m, width), jnp.float32),
     )(lhs, flats, mean)
 

time: 263 us -> 262 us (level)
  no operation moved by 1% of the time
where the time goes in v3:
time: 262 us
  blocking collectives  104 us (40%)
  waiting for transfers between devices  45.2 us (17%)
  other arithmetic  29.2 us (11%)
  Pallas kernels  22.2 us (8%)
  starting transfers between devices  17.1 us (7%)
  matrix products  17.1 us (7%)
  local copies, waits for them, and re-layouts  13.8 us (5%)
  between operations  13.6 us (5%)
    all_to_all x1, blocking collectives, shards(): back = lax.all_to_all(tiles_out, 'pix', 0, 0, tiled=True)  55.3 us
    all_to_all x1, waiting for transfers between devices, shards(): tiles = lax.all_to_all(tiles_in, 'pix', 0, 0, tiled=True)  36.4 us
    all_to_all x1, blocking collectives, sum_by_exchange(): lax.all_to_all(rows.reshape(count, total // count, width), axes, 0, 0, ti...  22.2 us
    all_to_all x1, blocking collectives, sum_by_exchange(): gathered = lax.all_to_all(spread, axes, 0, 0, tiled=True)  15.2 us
    pallas_call x1, Pallas kernels, frame_gram(): pl.pallas_call(_gram_kernel, grid=(cols // width,), in_specs=[pl.BlockSpe...  13.7 us
    all_gather x1, blocking collectives, shards(): mean_rows = lax.all_gather(mean_flat, 'ang', axis=1, tiled=True)  10.7 us
    another operation x6, other arithmetic, orthonormal(): lower = jnp.linalg.cholesky(correlation)  10.1 us
    another operation x4, other arithmetic, orthonormal(): return jax.scipy.linalg.solve_triangular(lower, grown.T, lower=True).T  8.65 us
  transfers between devices with their start and end apart: 4, of which 3 were waited for; matrix products, arithmetic and copies ran while one was open for 6% of the time, Pallas kernels for 0%

profile of v3, /device:TPU:1, one launch (start us, length us, event | category | flops | bytes accessed | tf_op | source)
XLA Modules:
  0.0 261.9 jit_solution(11869909333996625052)
XLA Ops:
  6.5 0.0 copy-start
  6.5 0.0 all-gather.2.cloned.1.call-start
  6.5 13.7 %shard_map.37 = (f32[256,256]{1,0:T(8,128)}, f32[8,1024]{1,0:T(8,128)}) custom-call(f32[256,8,1024]{2,1,0:T(8,128)} %flats_ref.3), custom_call_target="tpu_custom_call" | custom-call | tf_op jit(solution)/shard_map/pallas_call | solution.py:55
  20.2 1.2 reshape_reshape.5
  21.5 22.2 %all_to_all.30 = f32[128,1,512]{2,1,0:T(1,128)S(1)} all-to-all(f32[128,1,512]{2,1,0:T(1,128)S(1)} %reshape_reshape.5), channel_id=1, replica_groups=mesh['ang'=4,'pix'=32] {'ang','pix'}, dimensions={0} | all-to-all | bytes 524288 | tf_op jit(solution)/shard_map/all_to_all | solution.py:26
  43.7 0.2 reduce_sum.18
  43.9 0.1 broadcast_in_dim.4
  44.1 15.2 %all_to_all.31 = f32[128,1,512]{2,1,0:T(1,128)S(1)} all-to-all(f32[128,1,512]{2,1,0:T(1,128)S(1)} %broadcast_in_dim.4), channel_id=1, replica_groups=mesh['ang'=4,'pix'=32] {'ang','pix'}, dimensions={0} | all-to-all | bytes 524288 | tf_op jit(solution)/shard_map/all_to_all | solution.py:29
  59.3 0.7 multiply_reduce_fusion
  60.0 0.0 copy-done
  60.1 0.4 fusion.28
  60.4 0.2 fusion.29
  60.6 0.1 copy.23
  60.7 4.4 %cholesky.59 = f32[48,48]{1,0:T(8,128)S(1)} custom-call(f32[48,48]{1,0:T(8,128)S(1)} %fusion.25), custom_call_target="Cholesky" | custom-call | tf_op jit(solution)/shard_map/jit(cholesky)/cholesky | solution.py:15
  65.1 0.6 compare_reduce_fusion.2
  65.8 0.7 fusion.15
  66.4 3.7 %custom-call.14 = f32[1,48,48]{1,2,0:T(8,128)S(1)} custom-call(f32[1,48,48]{2,1,0:T(8,128)S(1)} %fusion.15), custom_call_target="InvertDiagBlocksLowerTriangular" | custom-call | tf_op jit(solution)/shard_map/jit(_solve_triangular)/triangular_solve | solution.py:16
  70.1 0.2 fusion.13
  70.3 0.4 fusion.30
  70.7 0.2 fusion.31
  70.9 0.1 copy.24
  71.0 4.4 %cholesky.70 = f32[48,48]{1,0:T(8,128)S(1)} custom-call(f32[48,48]{1,0:T(8,128)S(1)} %fusion.23), custom_call_target="Cholesky" | custom-call | tf_op jit(solution)/shard_map/jit(cholesky)/cholesky | solution.py:15
  75.4 0.6 compare_reduce_fusion.1
  76.0 0.7 fusion.16
  76.7 3.7 %custom-call.15 = f32[1,48,48]{1,2,0:T(8,128)S(1)} custom-call(f32[1,48,48]{2,1,0:T(8,128)S(1)} %fusion.16), custom_call_target="InvertDiagBlocksLowerTriangular" | custom-call | tf_op jit(solution)/shard_map/jit(_solve_triangular)/triangular_solve | solution.py:16
  80.4 0.9 fusion.11.lhs_ref
  81.3 8.5 %shard_map.38 = f32[8,48,1024]{2,1,0:T(8,128)} custom-call(f32[48,256]{1,0:T(8,128)} %fusion.11.lhs_ref, f32[256,8,1024]{2,1,0:T(8,128)} %flats_ref.3, f32[8,1024]{1,0:T(8,128)} %get-tuple-element.9.mean_ref), custom_call_target="tpu_custom_call" | custom-call | tf_op jit(solution)/shard_map/pallas_call | solution.py:83
  89.8 0.0 all-gather.2.cloned.1.call-update
  89.8 6.6 %copy.20 = f32[32,32,8,128]{3,1,2,0:T(8,128)} copy(f32[32,32,8,128]{3,2,0,1:T(8,128)} %bitcast.95) | data formatting | bytes 8388608 | tf_op jit(solution)/shard_map/transpose | solution.py:103
  96.4 0.0 copy-start.2
  96.4 0.0 copy-start.1
  96.4 5.7 %all-to-all-start = ((f32[32,32,8,128]{3,1,2,0:T(8,128)}), f32[32,32,8,128]{3,1,2,0:T(8,128)}, u32[]{:S(2)}, u32[]{:S(2)}) async-start(f32[32,32,8,128]{3,1,2,0:T(8,128)} %copy.20), calls=%async_computation | async-start | bytes 8388608 | tf_op jit(solution)/shard_map/all_to_all | solution.py:104
  102.1 0.0 copy-done.2
  102.1 10.7 %all_gather.6 = f32[8,4096]{1,0:T(8,128)S(1)} all-gather(f32[8,1024]{1,0:T(8,128)S(1)} %copy-done.2), channel_id=1, replica_groups=mesh['ang'=4,'pix'=32] {'ang'}, dimensions={1}, use_global_device_ids=true | all-gather | bytes 163840 | tf_op jit(solution)/shard_map/all_gather | solution.py:123
  112.9 0.0 copy-done.1
  112.9 0.4 fusion.32
  113.3 0.2 fusion.33
  113.4 0.1 copy.25
  113.5 4.4 %cholesky.81 = f32[48,48]{1,0:T(8,128)S(1)} custom-call(f32[48,48]{1,0:T(8,128)S(1)} %fusion.21), custom_call_target="Cholesky" | custom-call | tf_op jit(solution)/shard_map/jit(cholesky)/cholesky | solution.py:20
  118.0 36.4 %all-to-all-done = f32[32,32,8,128]{3,1,2,0:T(8,128)} async-done(((f32[32,32,8,128]{3,1,2,0:T(8,128)}), f32[32,32,8,128]{3,1,2,0:T(8,128)}, u32[]{:S(2)}, u32[]{:S(2)}) %all-to-all-start) | async-done | bytes 4194336 | tf_op jit(solution)/shard_map/all_to_all | solution.py:104
  154.4 0.0 all-gather.2.cloned.1.call-done
  154.4 7.5 %fusion = f32[32,48,1,1]{1,0,3,2:T(8,128)} fusion(f32[8,48,4096]{2,1,0:T(8,128)} %all-gather.2.cloned.1.call-done, f32[32,32,8,128]{3,1,2,0:T(8,128)} %all-to-all-done, f32[32,8,128]{2,0,1:T(8,128)S(1)} %copy.21), kind=kOutput, calls=%fused_computation | convolution fusion | flops 303038464 | bytes 10622976 | tf_op jit(solution)/shard_map/pjrc,rkpc->jk/dot_general | solution.py:127
  161.9 7.3 %all-to-all-start.3 = ((f32[32,1,48]{2,1,0:T(1,128)}), f32[32,1,48]{2,1,0:T(1,128)S(1)}, u32[]{:S(2)}, u32[]{:S(2)}) async-start(f32[32,1,48]{2,1,0:T(1,128)} %bitcast.18), calls=%async_computation.3 | async-start | bytes 32768 | tf_op jit(solution)/shard_map/all_to_all | solution.py:26
  169.2 0.7 compare_reduce_fusion
  169.9 6.2 %all-to-all-done.3 = f32[32,1,48]{2,1,0:T(1,128)S(1)} async-done(((f32[32,1,48]{2,1,0:T(1,128)}), f32[32,1,48]{2,1,0:T(1,128)S(1)}, u32[]{:S(2)}, u32[]{:S(2)}) %all-to-all-start.3) | async-done | bytes 6176 | tf_op jit(solution)/shard_map/all_to_all | solution.py:26
  176.1 0.1 reduce_sum.19
  176.1 0.6 broadcast_in_dim.6
  176.8 4.1 %all-to-all-start.4 = ((f32[32,1,48]{2,1,0:T(1,128)}), f32[32,1,48]{2,1,0:T(1,128)S(1)}, u32[]{:S(2)}, u32[]{:S(2)}) async-start(f32[32,1,48]{2,1,0:T(1,128)} %broadcast_in_dim.6), calls=%async_computation.4 | async-start | bytes 32768 | tf_op jit(solution)/shard_map/all_to_all | solution.py:29
  180.9 0.7 fusion.17
  181.6 3.7 %custom-call.12 = f32[1,48,48]{1,2,0:T(8,128)S(1)} custom-call(f32[1,48,48]{2,1,0:T(8,128)S(1)} %fusion.17), custom_call_target="InvertDiagBlocksLowerTriangular" | custom-call | tf_op jit(solution)/shard_map/jit(_cho_solve)/triangular_solve | solution.py:21
  185.3 2.6 %all-to-all-done.4 = f32[32,1,48]{2,1,0:T(1,128)S(1)} async-done(((f32[32,1,48]{2,1,0:T(1,128)}), f32[32,1,48]{2,1,0:T(1,128)S(1)}, u32[]{:S(2)}, u32[]{:S(2)}) %all-to-all-start.4) | async-done | bytes 6176 | tf_op jit(solution)/shard_map/all_to_all | solution.py:29
  187.9 0.1 fusion.19
  188.0 0.2 convolution_bitcast_fusion
  188.2 6.6 %fusion.7 = f32[32,32,8,128]{3,1,0,2:T(8,128)S(1)} fusion(f32[32,32,8,128]{3,1,2,0:T(8,128)} %all-to-all-done, f32[48,32,1,1]{0,1,3,2:T(8,128)S(1)} %convolution_bitcast_fusion, f32[32,8,128]{2,0,1:T(8,128)S(1)} %copy.21, f32[8,48,4096]{2,1,0:T(8,128)} %all-gather.2.cloned.1.call-done), kind=kOutput, calls=%fused_computation.8 | convolution fusion | flops 305135616 | bytes 14817280 | tf_op jit(solution)/shard_map/jk,rkpc->pjrc/dot_general | solution.py:132
  194.8 0.5 copy.32
  195.3 55.3 %all_to_all.32 = f32[32,32,8,128]{3,1,2,0:T(8,128)S(1)} all-to-all(f32[32,32,8,128]{3,1,2,0:T(8,128)S(1)} %copy.32), channel_id=1, replica_groups=mesh['ang'=4,'pix'=32] {'pix'}, dimensions={0} | all-to-all | bytes 8388608 | tf_op jit(solution)/shard_map/all_to_all | solution.py:136
  250.6 4.4 %copy.55 = f32[32,32,8,128]{3,2,0,1:T(8,128)} copy(f32[32,32,8,128]{3,1,2,0:T(8,128)S(1)} %all_to_all.32) | data formatting | bytes 8388608 | tf_op jit(solution)/shard_map/all_to_all | solution.py:136
  (9 shorter events, 0.2 us)
Async XLA Ops:
  6.5 53.5 %copy-start = (f32[256,48]{0,1:T(8,128)S(1)}, f32[256,48]{0,1:T(8,128)}, u32[]{:S(2)}) copy-start(f32[256,48]{0,1:T(8,128)} %param.8) | copy-start | bytes 147460
  6.5 147.8 %all-gather.2.cloned.1.call-start = ((), (), s32[]{:S(2)}) async-start(), calls=%async_computation.6 | async-start | bytes 7864320 | tf_op jit(solution)/shard_map/all_gather | solution.py:120
  96.4 5.7 %copy-start.2 = (f32[8,1024]{1,0:T(8,128)S(1)}, f32[8,1024]{1,0:T(8,128)}, u32[]{:S(2)}) copy-start(f32[8,1024]{1,0:T(8,128)} %get-tuple-element.9.mean_ref) | copy-start | bytes 98308
  96.4 16.5 %copy-start.1 = (f32[48,256]{1,0:T(8,128)S(1)}, f32[48,256]{1,0:T(8,128)}, u32[]{:S(2)}) copy-start(f32[48,256]{1,0:T(8,128)} %fusion.11.lhs_ref) | copy-start | bytes 147460
  96.4 57.9 %all-to-all-start = ((f32[32,32,8,128]{3,1,2,0:T(8,128)}), f32[32,32,8,128]{3,1,2,0:T(8,128)}, u32[]{:S(2)}, u32[]{:S(2)}) async-start(f32[32,32,8,128]{3,1,2,0:T(8,128)} %copy.20), calls=%async_computation | async-start | bytes 8388608 | tf_op jit(solution)/shard_map/all_to_all | solution.py:104
  161.9 14.2 %all-to-all-start.3 = ((f32[32,1,48]{2,1,0:T(1,128)}), f32[32,1,48]{2,1,0:T(1,128)S(1)}, u32[]{:S(2)}, u32[]{:S(2)}) async-start(f32[32,1,48]{2,1,0:T(1,128)} %bitcast.18), calls=%async_computation.3 | async-start | bytes 32768 | tf_op jit(solution)/shard_map/all_to_all | solution.py:26
  176.8 11.1 %all-to-all-start.4 = ((f32[32,1,48]{2,1,0:T(1,128)}), f32[32,1,48]{2,1,0:T(1,128)S(1)}, u32[]{:S(2)}, u32[]{:S(2)}) async-start(f32[32,1,48]{2,1,0:T(1,128)} %broadcast_in_dim.6), calls=%async_computation.4 | async-start | bytes 32768 | tf_op jit(solution)/shard_map/all_to_all | solution.py:29
Sparse Core Ops, SparseCore 0:
  89.9 62.9 all-gather.1

commit v4 on v2

--- a/solution.py
+++ b/solution.py
@@ -30,41 +30,55 @@
     return gathered.reshape(total, width)
 
 
-def _gram_kernel(flats_ref, gram_ref, mean_ref):
+def _gram_kernel(flats_ref, upper_ref, lower_ref, mean_ref):
     step = pl.program_id(0)
 
     @pl.when(step == 0)
     def _():
-        gram_ref[...] = jnp.zeros_like(gram_ref)
+        upper_ref[...] = jnp.zeros_like(upper_ref)
+        lower_ref[...] = jnp.zeros_like(lower_ref)
 
     block = flats_ref[...]
+    split = upper_ref.shape[0]
     mean = jnp.sum(block, axis=0) / block.shape[0]
     mean_ref[...] = mean
-    total = gram_ref[...]
+    upper = upper_ref[...]
+    lower = lower_ref[...]
+    pair = (((1,), (1,)), ((), ()))
     for row in range(block.shape[1]):
         centred = block[:, row, :] - mean[row][None, :]
-        total += lax.dot_general(
-            centred, centred, (((1,), (1,)), ((), ())),
+        upper += lax.dot_general(
+            centred[:split], centred, pair,
             precision=lax.Precision.HIGHEST, preferred_element_type=jnp.float32,
         )
-    gram_ref[...] = total
+        lower += lax.dot_general(
+            centred[split:], centred[split:], pair,
+            precision=lax.Precision.HIGHEST, preferred_element_type=jnp.float32,
+        )
+    upper_ref[...] = upper
+    lower_ref[...] = lower
 
 
 def frame_gram(flats, width=256):
     frames, rows, cols = flats.shape
-    return pl.pallas_call(
+    split = frames // 2
+    upper, lower, mean = pl.pallas_call(
         _gram_kernel,
         grid=(cols // width,),
         in_specs=[pl.BlockSpec((frames, rows, width), lambda i: (0, 0, i))],
         out_specs=[
-            pl.BlockSpec((frames, frames), lambda i: (0, 0)),
+            pl.BlockSpec((split, frames), lambda i: (0, 0)),
+            pl.BlockSpec((frames - split, frames - split), lambda i: (0, 0)),
             pl.BlockSpec((rows, width), lambda i: (0, i)),
         ],
         out_shape=[
-            jax.ShapeDtypeStruct((frames, frames), jnp.float32),
+            jax.ShapeDtypeStruct((split, frames), jnp.float32),
+            jax.ShapeDtypeStruct((frames - split, frames - split), jnp.float32),
             jax.ShapeDtypeStruct((rows, cols), jnp.float32),
         ],
     )(flats)
+    below = jnp.concatenate([upper[:, split:].T, lower], axis=1)
+    return jnp.concatenate([upper, below], axis=0), mean
 
 
 def _project_kernel(lhs_ref, flats_ref, mean_ref, out_ref):

time: 263 us -> 266 us (1.011)
  no operation moved by 1% of the time
where the time goes in v4:
time: 266 us; the launch traced here: 265 us
  blocking collectives  104 us (39%)
  waiting for transfers between devices  45 us (17%)
  other arithmetic  30.2 us (11%)
  Pallas kernels  25 us (9%)
  matrix products  17.1 us (6%)
  starting transfers between devices  16.9 us (6%)
  local copies, waits for them, and re-layouts  13.9 us (5%)
  between operations  13.6 us (5%)
    all_to_all x1, blocking collectives, shards(): back = lax.all_to_all(tiles_out, 'pix', 0, 0, tiled=True)  55.3 us
    all_to_all x1, waiting for transfers between devices, shards(): tiles = lax.all_to_all(tiles_in, 'pix', 0, 0, tiled=True)  36.2 us
    all_to_all x1, blocking collectives, sum_by_exchange(): lax.all_to_all(rows.reshape(count, total // count, width), axes, 0, 0, ti...  22.2 us
    pallas_call x1, Pallas kernels, frame_gram(): pl.pallas_call(_gram_kernel, grid=(cols // width,), in_specs=[pl.BlockSpe...  16 us
    all_to_all x1, blocking collectives, sum_by_exchange(): gathered = lax.all_to_all(spread, axes, 0, 0, tiled=True)  15.2 us
    all_gather x1, blocking collectives, shards(): mean_rows = lax.all_gather(mean_flat, 'ang', axis=1, tiled=True)  11 us
    another operation x6, other arithmetic, orthonormal(): lower = jnp.linalg.cholesky(correlation)  10.1 us
    pallas_call x1, Pallas kernels, project_rows(): pl.pallas_call(_project_kernel, grid=(1,), in_specs=[pl.BlockSpec((m, k),...  8.96 us
  transfers between devices with their start and end apart: 4, of which 3 were waited for; matrix products, arithmetic and copies ran while one was open for 6% of the time, Pallas kernels for 0%

profile of v4, /device:TPU:1, one launch (start us, length us, event | category | flops | bytes accessed | tf_op | source)
XLA Modules:
  0.0 265.5 jit_solution(10835623618162796991)
XLA Ops:
  6.5 0.0 copy-start
  6.5 0.0 all-gather.2.cloned.1.call-start
  6.5 16.0 %shard_map.37 = (f32[128,256]{1,0:T(8,128)}, f32[128,128]{1,0:T(8,128)}, f32[8,1024]{1,0:T(8,128)}) custom-call(f32[256,8,1024]{2,1,0:T(8,128)} %flats_ref.3), custom_call_target="tpu_custom_call" | custom-call | tf_op jit(solution)/shard_map/pallas_call | solution.py:65
  22.6 1.0 copy.24
  23.6 1.0 maximum_maximum_fusion
  24.6 0.3 reshape_reshape.5
  24.8 22.2 %all_to_all.30 = f32[128,1,512]{2,1,0:T(1,128)S(1)} all-to-all(f32[128,1,512]{2,1,0:T(1,128)S(1)} %reshape_reshape.5), channel_id=1, replica_groups=mesh['ang'=4,'pix'=32] {'ang','pix'}, dimensions={0} | all-to-all | bytes 524288 | tf_op jit(solution)/shard_map/all_to_all | solution.py:26
  47.1 0.2 reduce_sum.18
  47.3 0.1 broadcast_in_dim.4
  47.4 15.2 %all_to_all.31 = f32[128,1,512]{2,1,0:T(1,128)S(1)} all-to-all(f32[128,1,512]{2,1,0:T(1,128)S(1)} %broadcast_in_dim.4), channel_id=1, replica_groups=mesh['ang'=4,'pix'=32] {'ang','pix'}, dimensions={0} | all-to-all | bytes 524288 | tf_op jit(solution)/shard_map/all_to_all | solution.py:29
  62.6 0.7 multiply_reduce_fusion
  63.4 0.0 copy-done
  63.4 0.4 fusion.28
  63.8 0.2 fusion.29
  64.0 0.1 copy.26
  64.1 4.4 %cholesky.59 = f32[48,48]{1,0:T(8,128)S(1)} custom-call(f32[48,48]{1,0:T(8,128)S(1)} %fusion.25), custom_call_target="Cholesky" | custom-call | tf_op jit(solution)/shard_map/jit(cholesky)/cholesky | solution.py:15
  68.5 0.6 compare_reduce_fusion.2
  69.1 0.7 fusion.15
  69.8 3.7 %custom-call.14 = f32[1,48,48]{1,2,0:T(8,128)S(1)} custom-call(f32[1,48,48]{2,1,0:T(8,128)S(1)} %fusion.15), custom_call_target="InvertDiagBlocksLowerTriangular" | custom-call | tf_op jit(solution)/shard_map/jit(_solve_triangular)/triangular_solve | solution.py:16
  73.4 0.2 fusion.13
  73.7 0.4 fusion.30
  74.1 0.2 fusion.31
  74.3 0.1 copy.27
  74.3 4.4 %cholesky.70 = f32[48,48]{1,0:T(8,128)S(1)} custom-call(f32[48,48]{1,0:T(8,128)S(1)} %fusion.23), custom_call_target="Cholesky" | custom-call | tf_op jit(solution)/shard_map/jit(cholesky)/cholesky | solution.py:15
  78.8 0.6 compare_reduce_fusion.1
  79.4 0.7 fusion.16
  80.1 3.7 %custom-call.15 = f32[1,48,48]{1,2,0:T(8,128)S(1)} custom-call(f32[1,48,48]{2,1,0:T(8,128)S(1)} %fusion.16), custom_call_target="InvertDiagBlocksLowerTriangular" | custom-call | tf_op jit(solution)/shard_map/jit(_solve_triangular)/triangular_solve | solution.py:16
  83.7 0.9 fusion.11.lhs_ref
  84.6 9.0 %shard_map.38 = f32[8,48,1024]{2,1,0:T(8,128)} custom-call(f32[48,256]{1,0:T(8,128)} %fusion.11.lhs_ref, f32[256,8,1024]{2,1,0:T(8,128)} %flats_ref.3, f32[8,1024]{1,0:T(8,128)} %get-tuple-element.10.mean_ref), custom_call_target="tpu_custom_call" | custom-call | tf_op jit(solution)/shard_map/pallas_call | solution.py:97
  93.6 0.0 all-gather.2.cloned.1.call-update
  93.6 6.6 %copy.22 = f32[32,32,8,128]{3,1,2,0:T(8,128)} copy(f32[32,32,8,128]{3,2,0,1:T(8,128)} %bitcast.97) | data formatting | bytes 8388608 | tf_op jit(solution)/shard_map/transpose | solution.py:117
  100.2 0.0 copy-start.2
  100.2 0.0 copy-start.1
  100.2 5.6 %all-to-all-start = ((f32[32,32,8,128]{3,1,2,0:T(8,128)}), f32[32,32,8,128]{3,1,2,0:T(8,128)}, u32[]{:S(2)}, u32[]{:S(2)}) async-start(f32[32,32,8,128]{3,1,2,0:T(8,128)} %copy.22), calls=%async_computation | async-start | bytes 8388608 | tf_op jit(solution)/shard_map/all_to_all | solution.py:118
  105.9 0.0 copy-done.2
  105.9 11.0 %all_gather.6 = f32[8,4096]{1,0:T(8,128)S(1)} all-gather(f32[8,1024]{1,0:T(8,128)S(1)} %copy-done.2), channel_id=1, replica_groups=mesh['ang'=4,'pix'=32] {'ang'}, dimensions={1}, use_global_device_ids=true | all-gather | bytes 163840 | tf_op jit(solution)/shard_map/all_gather | solution.py:137
  116.9 0.0 copy-done.1
  116.9 0.4 fusion.32
  117.3 0.2 fusion.33
  117.5 0.1 copy.28
  117.6 4.4 %cholesky.81 = f32[48,48]{1,0:T(8,128)S(1)} custom-call(f32[48,48]{1,0:T(8,128)S(1)} %fusion.21), custom_call_target="Cholesky" | custom-call | tf_op jit(solution)/shard_map/jit(cholesky)/cholesky | solution.py:20
  122.0 36.2 %all-to-all-done = f32[32,32,8,128]{3,1,2,0:T(8,128)} async-done(((f32[32,32,8,128]{3,1,2,0:T(8,128)}), f32[32,32,8,128]{3,1,2,0:T(8,128)}, u32[]{:S(2)}, u32[]{:S(2)}) %all-to-all-start) | async-done | bytes 4194336 | tf_op jit(solution)/shard_map/all_to_all | solution.py:118
  158.2 0.0 all-gather.2.cloned.1.call-done
  158.2 7.5 %fusion = f32[32,48,1,1]{1,0,3,2:T(8,128)} fusion(f32[8,48,4096]{2,1,0:T(8,128)} %all-gather.2.cloned.1.call-done, f32[32,32,8,128]{3,1,2,0:T(8,128)} %all-to-all-done, f32[32,8,128]{2,0,1:T(8,128)S(1)} %copy.23), kind=kOutput, calls=%fused_computation | convolution fusion | flops 303038464 | bytes 10622976 | tf_op jit(solution)/shard_map/pjrc,rkpc->jk/dot_general | solution.py:141
  165.6 7.1 %all-to-all-start.3 = ((f32[32,1,48]{2,1,0:T(1,128)}), f32[32,1,48]{2,1,0:T(1,128)S(1)}, u32[]{:S(2)}, u32[]{:S(2)}) async-start(f32[32,1,48]{2,1,0:T(1,128)} %bitcast.19), calls=%async_computation.3 | async-start | bytes 32768 | tf_op jit(solution)/shard_map/all_to_all | solution.py:26
  172.8 0.7 compare_reduce_fusion
  173.5 6.2 %all-to-all-done.3 = f32[32,1,48]{2,1,0:T(1,128)S(1)} async-done(((f32[32,1,48]{2,1,0:T(1,128)}), f32[32,1,48]{2,1,0:T(1,128)S(1)}, u32[]{:S(2)}, u32[]{:S(2)}) %all-to-all-start.3) | async-done | bytes 6176 | tf_op jit(solution)/shard_map/all_to_all | solution.py:26
  179.7 0.1 reduce_sum.19
  179.7 0.6 broadcast_in_dim.6
  180.3 4.1 %all-to-all-start.4 = ((f32[32,1,48]{2,1,0:T(1,128)}), f32[32,1,48]{2,1,0:T(1,128)S(1)}, u32[]{:S(2)}, u32[]{:S(2)}) async-start(f32[32,1,48]{2,1,0:T(1,128)} %broadcast_in_dim.6), calls=%async_computation.4 | async-start | bytes 32768 | tf_op jit(solution)/shard_map/all_to_all | solution.py:29
  184.5 0.7 fusion.17
  185.2 3.7 %custom-call.12 = f32[1,48,48]{1,2,0:T(8,128)S(1)} custom-call(f32[1,48,48]{2,1,0:T(8,128)S(1)} %fusion.17), custom_call_target="InvertDiagBlocksLowerTriangular" | custom-call | tf_op jit(solution)/shard_map/jit(_cho_solve)/triangular_solve | solution.py:21
  188.8 2.6 all-to-all-done.4
  191.5 0.1 fusion.19
  191.6 0.2 convolution_bitcast_fusion
  191.8 6.6 %fusion.7 = f32[32,32,8,128]{3,1,0,2:T(8,128)S(1)} fusion(f32[32,32,8,128]{3,1,2,0:T(8,128)} %all-to-all-done, f32[48,32,1,1]{0,1,3,2:T(8,128)S(1)} %convolution_bitcast_fusion, f32[32,8,128]{2,0,1:T(8,128)S(1)} %copy.23, f32[8,48,4096]{2,1,0:T(8,128)} %all-gather.2.cloned.1.call-done), kind=kOutput, calls=%fused_computation.8 | convolution fusion | flops 305135616 | bytes 14817280 | tf_op jit(solution)/shard_map/jk,rkpc->pjrc/dot_general | solution.py:146
  198.4 0.5 copy.35
  198.9 55.3 %all_to_all.32 = f32[32,32,8,128]{3,1,2,0:T(8,128)S(1)} all-to-all(f32[32,32,8,128]{3,1,2,0:T(8,128)S(1)} %copy.35), channel_id=1, replica_groups=mesh['ang'=4,'pix'=32] {'pix'}, dimensions={0} | all-to-all | bytes 8388608 | tf_op jit(solution)/shard_map/all_to_all | solution.py:150
  254.2 4.4 %copy.58 = f32[32,32,8,128]{3,2,0,1:T(8,128)} copy(f32[32,32,8,128]{3,1,2,0:T(8,128)S(1)} %all_to_all.32) | data formatting | bytes 8388608 | tf_op jit(solution)/shard_map/all_to_all | solution.py:150
  (10 shorter events, 0.2 us)
Async XLA Ops:
  6.5 56.9 %copy-start = (f32[256,48]{0,1:T(8,128)S(1)}, f32[256,48]{0,1:T(8,128)}, u32[]{:S(2)}) copy-start(f32[256,48]{0,1:T(8,128)} %param.8) | copy-start | bytes 147460
  6.5 151.6 %all-gather.2.cloned.1.call-start = ((), (), s32[]{:S(2)}) async-start(), calls=%async_computation.6 | async-start | bytes 7864320 | tf_op jit(solution)/shard_map/all_gather | solution.py:134
  100.2 5.7 %copy-start.2 = (f32[8,1024]{1,0:T(8,128)S(1)}, f32[8,1024]{1,0:T(8,128)}, u32[]{:S(2)}) copy-start(f32[8,1024]{1,0:T(8,128)} %get-tuple-element.10.mean_ref) | copy-start | bytes 98308
  100.2 16.7 %copy-start.1 = (f32[48,256]{1,0:T(8,128)S(1)}, f32[48,256]{1,0:T(8,128)}, u32[]{:S(2)}) copy-start(f32[48,256]{1,0:T(8,128)} %fusion.11.lhs_ref) | copy-start | bytes 147460
  100.2 57.9 %all-to-all-start = ((f32[32,32,8,128]{3,1,2,0:T(8,128)}), f32[32,32,8,128]{3,1,2,0:T(8,128)}, u32[]{:S(2)}, u32[]{:S(2)}) async-start(f32[32,32,8,128]{3,1,2,0:T(8,128)} %copy.22), calls=%async_computation | async-start | bytes 8388608 | tf_op jit(solution)/shard_map/all_to_all | solution.py:118
  165.6 14.0 %all-to-all-start.3 = ((f32[32,1,48]{2,1,0:T(1,128)}), f32[32,1,48]{2,1,0:T(1,128)S(1)}, u32[]{:S(2)}, u32[]{:S(2)}) async-start(f32[32,1,48]{2,1,0:T(1,128)} %bitcast.19), calls=%async_computation.3 | async-start | bytes 32768 | tf_op jit(solution)/shard_map/all_to_all | solution.py:26
  180.3 11.1 %all-to-all-start.4 = ((f32[32,1,48]{2,1,0:T(1,128)}), f32[32,1,48]{2,1,0:T(1,128)S(1)}, u32[]{:S(2)}, u32[]{:S(2)}) async-start(f32[32,1,48]{2,1,0:T(1,128)} %broadcast_in_dim.6), calls=%async_computation.4 | async-start | bytes 32768 | tf_op jit(solution)/shard_map/all_to_all | solution.py:29
Sparse Core Ops, SparseCore 0:
  93.7 62.9 all-gather.1

commit v5 on v2

--- a/solution.py
+++ b/solution.py
@@ -129,12 +129,16 @@
     )
     fit_rhs = sum_by_exchange(partial_value, "pix", pix_count) / npix
     weights = solve_normal(normal, fit_rhs)
-    estimate = mean_blk.transpose(1, 0, 2)[:, None] + jnp.einsum(
-        "jk,rkpc->pjrc", weights, eigen_blk, precision=lax.Precision.HIGH
-    )
-    tiles_out = tiles / jnp.maximum(estimate, floor_value)
-    back = lax.all_to_all(tiles_out, "pix", 0, 0, tiled=True)
-    result = back.transpose(1, 0, 2, 3).reshape(angle_count, rows_all, cols_here)
+    halves = []
+    share = angle_count // 2
+    for first in (0, share):
+        estimate = mean_blk.transpose(1, 0, 2)[:, None] + jnp.einsum(
+            "jk,rkpc->pjrc", weights[first:first + share], eigen_blk, precision=lax.Precision.HIGH
+        )
+        part = tiles[:, first:first + share] / jnp.maximum(estimate, floor_value)
+        back = lax.all_to_all(part, "pix", 0, 0, tiled=True)
+        halves.append(back.transpose(1, 0, 2, 3).reshape(share, rows_all, cols_here))
+    result = jnp.concatenate(halves, axis=0)
     return result
 
 

time: 263 us -> 273 us (1.038)
  blocking collectives: 104 us -> 48.4 us
  waiting for transfers between devices: 45 us -> 89.1 us
  starting transfers between devices: 16.9 us -> 27.3 us
  local copies, waits for them, and re-layouts: 13.8 us -> 20.3 us
    all_to_all x1 -> x0, blocking collectives: 55.3 us -> none  [shards(): back = lax.all_to_all(tiles_out, 'pix', 0, 0, tiled=True)]
    all_to_all x0 -> x2, waiting for transfers between devices: none -> 48.2 us  [shards(): back = lax.all_to_all(part, 'pix', 0, 0, tiled=True)]
    all_to_all x0 -> x2, starting transfers between devices: none -> 9.64 us  [shards(): back = lax.all_to_all(part, 'pix', 0, 0, tiled=True)]
    slice x0 -> x1, local copies, waits for them, and re-layouts: none -> 3.99 us  [shards(): part = tiles[:, first:first + share] / jnp.maximum(estimate, floor_value)]
    all_to_all x1, waiting for transfers between devices: 6.17 us -> 2.51 us  [sum_by_exchange(): lax.all_to_all(rows.reshape(count, total // count, width), axes, 0, 0, ti...]
    div x1 -> x2, local copies, waits for them, and re-layouts: 0.48 us -> 3.23 us  [shards(): part = tiles[:, first:first + share] / jnp.maximum(estimate, floor_value)]
    dot_general x1 -> x2, matrix products: 6.59 us -> 8.76 us  [shards(): jnp.einsum('jk,rkpc->pjrc', weights[first:first + share], eigen_blk, prec...]
  transfers between devices with their start and end apart: 4 -> 6, of which waited for: 3 -> 5; matrix products, arithmetic and copies ran while one was open for 6% -> 11% of each run, Pallas kernels for 0% -> 0%
where the time goes in v5:
time: 273 us; the launch traced here: 272 us
  waiting for transfers between devices  89.1 us (33%)
  blocking collectives  48.4 us (18%)
  other arithmetic  31.7 us (12%)
  starting transfers between devices  27.3 us (10%)
  Pallas kernels  22.7 us (8%)
  local copies, waits for them, and re-layouts  20.3 us (7%)
  matrix products  19.3 us (7%)
  between operations  13.7 us (5%)
    all_to_all x2, waiting for transfers between devices, shards(): back = lax.all_to_all(part, 'pix', 0, 0, tiled=True)  48.2 us
    all_to_all x1, waiting for transfers between devices, shards(): tiles = lax.all_to_all(tiles_in, 'pix', 0, 0, tiled=True)  35.5 us
    all_to_all x1, blocking collectives, sum_by_exchange(): lax.all_to_all(rows.reshape(count, total // count, width), axes, 0, 0, ti...  22.2 us
    all_to_all x1, blocking collectives, sum_by_exchange(): gathered = lax.all_to_all(spread, axes, 0, 0, tiled=True)  15.2 us
    pallas_call x1, Pallas kernels, frame_gram(): pl.pallas_call(_gram_kernel, grid=(cols // width,), in_specs=[pl.BlockSpe...  13.7 us
    all_gather x1, blocking collectives, shards(): mean_rows = lax.all_gather(mean_flat, 'ang', axis=1, tiled=True)  11 us
    another operation x6, other arithmetic, orthonormal(): lower = jnp.linalg.cholesky(correlation)  10.1 us
    all_to_all x2, starting transfers between devices, shards(): back = lax.all_to_all(part, 'pix', 0, 0, tiled=True)  9.64 us
  transfers between devices with their start and end apart: 6, of which 5 were waited for; matrix products, arithmetic and copies ran while one was open for 11% of the time, Pallas kernels for 0%

profile of v5, /device:TPU:1, one launch (start us, length us, event | category | flops | bytes accessed | tf_op | source)
XLA Modules:
  0.0 272.4 jit_solution(7776537970554391938)
XLA Ops:
  6.5 0.0 copy-start
  6.5 0.0 all-gather.2.cloned.1.call-start
  6.5 13.7 %shard_map.37 = (f32[256,256]{1,0:T(8,128)}, f32[8,1024]{1,0:T(8,128)}) custom-call(f32[256,8,1024]{2,1,0:T(8,128)} %flats_ref.3), custom_call_target="tpu_custom_call" | custom-call | tf_op jit(solution)/shard_map/pallas_call | solution.py:55
  20.2 1.2 reshape_reshape.5
  21.5 22.2 %all_to_all.35 = f32[128,1,512]{2,1,0:T(1,128)S(1)} all-to-all(f32[128,1,512]{2,1,0:T(1,128)S(1)} %reshape_reshape.5), channel_id=1, replica_groups=mesh['ang'=4,'pix'=32] {'ang','pix'}, dimensions={0} | all-to-all | bytes 524288 | tf_op jit(solution)/shard_map/all_to_all | solution.py:26
  43.7 0.2 reduce_sum.18
  43.9 0.1 broadcast_in_dim.4
  44.1 15.2 %all_to_all.36 = f32[128,1,512]{2,1,0:T(1,128)S(1)} all-to-all(f32[128,1,512]{2,1,0:T(1,128)S(1)} %broadcast_in_dim.4), channel_id=1, replica_groups=mesh['ang'=4,'pix'=32] {'ang','pix'}, dimensions={0} | all-to-all | bytes 524288 | tf_op jit(solution)/shard_map/all_to_all | solution.py:29
  59.3 0.7 multiply_reduce_fusion
  60.0 0.0 copy-done
  60.1 0.4 fusion.36
  60.4 0.2 fusion.37
  60.6 0.1 copy.29
  60.7 4.4 %cholesky.59 = f32[48,48]{1,0:T(8,128)S(1)} custom-call(f32[48,48]{1,0:T(8,128)S(1)} %fusion.32), custom_call_target="Cholesky" | custom-call | tf_op jit(solution)/shard_map/jit(cholesky)/cholesky | solution.py:15
  65.1 0.6 compare_reduce_fusion.2
  65.8 0.7 fusion.21
  66.4 3.7 %custom-call.14 = f32[1,48,48]{1,2,0:T(8,128)S(1)} custom-call(f32[1,48,48]{2,1,0:T(8,128)S(1)} %fusion.21), custom_call_target="InvertDiagBlocksLowerTriangular" | custom-call | tf_op jit(solution)/shard_map/jit(_solve_triangular)/triangular_solve | solution.py:16
  70.1 0.2 fusion.19
  70.3 0.4 fusion.38
  70.7 0.2 fusion.39
  70.9 0.1 copy.30
  71.0 4.4 %cholesky.70 = f32[48,48]{1,0:T(8,128)S(1)} custom-call(f32[48,48]{1,0:T(8,128)S(1)} %fusion.30), custom_call_target="Cholesky" | custom-call | tf_op jit(solution)/shard_map/jit(cholesky)/cholesky | solution.py:15
  75.4 0.6 compare_reduce_fusion.1
  76.0 0.7 fusion.22
  76.7 3.7 %custom-call.15 = f32[1,48,48]{1,2,0:T(8,128)S(1)} custom-call(f32[1,48,48]{2,1,0:T(8,128)S(1)} %fusion.22), custom_call_target="InvertDiagBlocksLowerTriangular" | custom-call | tf_op jit(solution)/shard_map/jit(_solve_triangular)/triangular_solve | solution.py:16
  80.4 0.9 fusion.17.lhs_ref
  81.3 9.0 %shard_map.38 = f32[8,48,1024]{2,1,0:T(8,128)} custom-call(f32[48,256]{1,0:T(8,128)} %fusion.17.lhs_ref, f32[256,8,1024]{2,1,0:T(8,128)} %flats_ref.3, f32[8,1024]{1,0:T(8,128)} %get-tuple-element.9.mean_ref), custom_call_target="tpu_custom_call" | custom-call | tf_op jit(solution)/shard_map/pallas_call | solution.py:83
  90.2 0.0 all-gather.2.cloned.1.call-update
  90.2 6.6 %copy.25 = f32[32,32,8,128]{3,1,2,0:T(8,128)} copy(f32[32,32,8,128]{3,2,0,1:T(8,128)} %bitcast.120) | data formatting | bytes 8388608 | tf_op jit(solution)/shard_map/transpose | solution.py:103
  96.9 0.0 copy-start.3
  96.9 5.7 %all-to-all-start = ((f32[32,32,8,128]{3,1,2,0:T(8,128)}), f32[32,32,8,128]{3,1,2,0:T(8,128)}, u32[]{:S(2)}, u32[]{:S(2)}) async-start(f32[32,32,8,128]{3,1,2,0:T(8,128)} %copy.25), calls=%async_computation | async-start | bytes 8388608 | tf_op jit(solution)/shard_map/all_to_all | solution.py:104
  102.5 0.0 copy-done.3
  102.5 11.0 %all_gather.6 = f32[8,4096]{1,0:T(8,128)S(1)} all-gather(f32[8,1024]{1,0:T(8,128)S(1)} %copy-done.3), channel_id=1, replica_groups=mesh['ang'=4,'pix'=32] {'ang'}, dimensions={1}, use_global_device_ids=true | all-gather | bytes 163840 | tf_op jit(solution)/shard_map/all_gather | solution.py:123
  113.5 0.0 copy-done.2
  113.6 0.4 fusion.40
  113.9 0.2 fusion.41
  114.1 0.1 copy.31
  114.2 4.4 %cholesky.81 = f32[48,48]{1,0:T(8,128)S(1)} custom-call(f32[48,48]{1,0:T(8,128)S(1)} %fusion.28), custom_call_target="Cholesky" | custom-call | tf_op jit(solution)/shard_map/jit(cholesky)/cholesky | solution.py:20
  118.6 0.7 compare_reduce_fusion
  119.3 35.5 %all-to-all-done = f32[32,32,8,128]{3,1,2,0:T(8,128)} async-done(((f32[32,32,8,128]{3,1,2,0:T(8,128)}), f32[32,32,8,128]{3,1,2,0:T(8,128)}, u32[]{:S(2)}, u32[]{:S(2)}) %all-to-all-start) | async-done | bytes 4194336 | tf_op jit(solution)/shard_map/all_to_all | solution.py:104
  154.8 7.5 %fusion = f32[32,48,1,1]{1,0,3,2:T(8,128)} fusion(f32[32,32,8,128]{3,1,2,0:T(8,128)} %all-to-all-done, f32[32,8,128]{2,1,0:T(8,128)S(1)} %bitcast.122, f32[8,48,4096]{2,1,0:T(8,128)} %all-gather.2.cloned.1.call-done), kind=kOutput, calls=%fused_computation | convolution fusion | flops 303038464 | bytes 10622976 | tf_op jit(solution)/shard_map/pjrc,rkpc->jk/dot_general | solution.py:127
  162.3 7.1 %all-to-all-start.3 = ((f32[32,1,48]{2,1,0:T(1,128)}), f32[32,1,48]{2,1,0:T(1,128)S(1)}, u32[]{:S(2)}, u32[]{:S(2)}) async-start(f32[32,1,48]{2,1,0:T(1,128)} %bitcast.19), calls=%async_computation.3 | async-start | bytes 32768 | tf_op jit(solution)/shard_map/all_to_all | solution.py:26
  169.4 0.7 fusion.23
  170.1 3.7 %custom-call.12 = f32[1,48,48]{1,2,0:T(8,128)S(1)} custom-call(f32[1,48,48]{2,1,0:T(8,128)S(1)} %fusion.23), custom_call_target="InvertDiagBlocksLowerTriangular" | custom-call | tf_op jit(solution)/shard_map/jit(_cho_solve)/triangular_solve | solution.py:21
  173.8 2.5 all-to-all-done.3
  176.3 0.1 reduce_sum.19
  176.4 0.6 broadcast_in_dim.6
  177.0 4.9 %all-to-all-start.4 = ((f32[32,1,48]{2,1,0:T(1,128)}), f32[32,1,48]{2,1,0:T(1,128)S(1)}, u32[]{:S(2)}, u32[]{:S(2)}) async-start(f32[32,1,48]{2,1,0:T(1,128)} %broadcast_in_dim.6), calls=%async_computation.4 | async-start | bytes 32768 | tf_op jit(solution)/shard_map/all_to_all | solution.py:29
  181.9 4.0 %fusion.35 = (f32[32,16,8,128]{3,1,2,0:T(8,128)S(1)}, f32[32,16,8,128]{3,1,2,0:T(8,128)}) fusion(f32[32,32,8,128]{3,1,2,0:T(8,128)} %all-to-all-done), kind=kLoop, calls=%fused_computation.55 | loop fusion | bytes 8388608 | tf_op jit(solution)/shard_map/slice | solution.py:138
  185.9 2.9 %all-to-all-done.4 = f32[32,1,48]{2,1,0:T(1,128)S(1)} async-done(((f32[32,1,48]{2,1,0:T(1,128)}), f32[32,1,48]{2,1,0:T(1,128)S(1)}, u32[]{:S(2)}, u32[]{:S(2)}) %all-to-all-start.4) | async-done | bytes 6176 | tf_op jit(solution)/shard_map/all_to_all | solution.py:29
  188.8 0.1 fusion.26
  189.0 0.2 fusion.24
  189.1 3.7 %copy_divide_fusion.1 = f32[32,16,8,128]{3,1,0,2:T(8,128)S(1)} fusion(f32[32,16,8,128]{3,1,2,0:T(8,128)S(1)} %get-tuple-element.11, f32[32,8,128]{2,0,1:T(8,128)S(1)} %copy.27, f32[32,48]{1,0:T(8,128)S(1)} %fusion.24, f32[8,48,4096]{2,1,0:T(8,128)} %all-gather.2.cloned.1.call-done), kind=kOutput, calls=%fused_computation.12 | convolution fusion | flops 152567808 | bytes 10625024 | tf_op jit(solution)/shard_map/jk,rkpc->pjrc/dot_general | solution.py:135
  192.9 1.6 copy.35
  194.5 4.4 %all-to-all-start.5 = ((f32[32,16,8,128]{3,1,2,0:T(8,128)}), f32[32,16,8,128]{3,1,2,0:T(8,128)S(1)}, u32[]{:S(2)}, u32[]{:S(2)}) async-start(f32[32,16,8,128]{3,1,2,0:T(8,128)} %copy.35), calls=%async_computation.5 | async-start | bytes 4194304 | tf_op jit(solution)/shard_map/all_to_all | solution.py:139
  199.0 5.0 %copy_divide_fusion = f32[32,16,8,128]{3,1,0,2:T(8,128)S(1)} fusion(f32[32,16,8,128]{3,1,2,0:T(8,128)} %get-tuple-element.12, f32[32,8,128]{2,0,1:T(8,128)S(1)} %copy.27, f32[32,48]{1,0:T(8,128)S(1)} %fusion.24, f32[8,48,4096]{2,1,0:T(8,128)} %all-gather.2.cloned.1.call-done), kind=kOutput, calls=%fused_computation.11 | convolution fusion | flops 152567808 | bytes 10625024 | tf_op jit(solution)/shard_map/jk,rkpc->pjrc/dot_general | solution.py:135
  204.0 1.6 copy.39
  205.6 21.7 %all-to-all-done.5 = f32[32,16,8,128]{3,1,2,0:T(8,128)S(1)} async-done(((f32[32,16,8,128]{3,1,2,0:T(8,128)}), f32[32,16,8,128]{3,1,2,0:T(8,128)S(1)}, u32[]{:S(2)}, u32[]{:S(2)}) %all-to-all-start.5) | async-done | bytes 2097184 | tf_op jit(solution)/shard_map/all_to_all | solution.py:139
  227.3 5.2 %all-to-all-start.6 = ((f32[32,16,8,128]{3,1,2,0:T(8,128)}), f32[32,16,8,128]{3,1,2,0:T(8,128)}, u32[]{:S(2)}, u32[]{:S(2)}) async-start(f32[32,16,8,128]{3,1,2,0:T(8,128)} %copy.39), calls=%async_computation.6 | async-start | bytes 4194304 | tf_op jit(solution)/shard_map/all_to_all | solution.py:139
  232.5 1.9 copy.69
  234.4 26.5 %all-to-all-done.6 = f32[32,16,8,128]{3,1,2,0:T(8,128)} async-done(((f32[32,16,8,128]{3,1,2,0:T(8,128)}), f32[32,16,8,128]{3,1,2,0:T(8,128)}, u32[]{:S(2)}, u32[]{:S(2)}) %all-to-all-start.6) | async-done | bytes 2097184 | tf_op jit(solution)/shard_map/all_to_all | solution.py:139
  260.9 2.3 copy.68
  263.2 0.0 copy-done.1
  263.2 2.4 pad_maximum_fusion
  (12 shorter events, 0.2 us)
Async XLA Ops:
  6.5 53.5 %copy-start = (f32[256,48]{0,1:T(8,128)S(1)}, f32[256,48]{0,1:T(8,128)}, u32[]{:S(2)}) copy-start(f32[256,48]{0,1:T(8,128)} %param.8) | copy-start | bytes 147460
  6.5 148.3 %all-gather.2.cloned.1.call-start = ((), (), s32[]{:S(2)}) async-start(), calls=%async_computation.7 | async-start | bytes 7864320 | tf_op jit(solution)/shard_map/all_gather | solution.py:120
  96.9 5.7 %copy-start.3 = (f32[8,1024]{1,0:T(8,128)S(1)}, f32[8,1024]{1,0:T(8,128)}, u32[]{:S(2)}) copy-start(f32[8,1024]{1,0:T(8,128)} %get-tuple-element.9.mean_ref) | copy-start | bytes 98308
  96.9 16.7 %copy-start.2 = (f32[48,256]{1,0:T(8,128)S(1)}, f32[48,256]{1,0:T(8,128)}, u32[]{:S(2)}) copy-start(f32[48,256]{1,0:T(8,128)} %fusion.17.lhs_ref) | copy-start | bytes 147460
  96.9 57.9 %all-to-all-start = ((f32[32,32,8,128]{3,1,2,0:T(8,128)}), f32[32,32,8,128]{3,1,2,0:T(8,128)}, u32[]{:S(2)}, u32[]{:S(2)}) async-start(f32[32,32,8,128]{3,1,2,0:T(8,128)} %copy.25), calls=%async_computation | async-start | bytes 8388608 | tf_op jit(solution)/shard_map/all_to_all | solution.py:104
  162.3 14.0 %all-to-all-start.3 = ((f32[32,1,48]{2,1,0:T(1,128)}), f32[32,1,48]{2,1,0:T(1,128)S(1)}, u32[]{:S(2)}, u32[]{:S(2)}) async-start(f32[32,1,48]{2,1,0:T(1,128)} %bitcast.19), calls=%async_computation.3 | async-start | bytes 32768 | tf_op jit(solution)/shard_map/all_to_all | solution.py:26
  177.0 11.8 %all-to-all-start.4 = ((f32[32,1,48]{2,1,0:T(1,128)}), f32[32,1,48]{2,1,0:T(1,128)S(1)}, u32[]{:S(2)}, u32[]{:S(2)}) async-start(f32[32,1,48]{2,1,0:T(1,128)} %broadcast_in_dim.6), calls=%async_computation.4 | async-start | bytes 32768 | tf_op jit(solution)/shard_map/all_to_all | solution.py:29
  194.5 32.7 %all-to-all-start.5 = ((f32[32,16,8,128]{3,1,2,0:T(8,128)}), f32[32,16,8,128]{3,1,2,0:T(8,128)S(1)}, u32[]{:S(2)}, u32[]{:S(2)}) async-start(f32[32,16,8,128]{3,1,2,0:T(8,128)} %copy.35), calls=%async_computation.5 | async-start | bytes 4194304 | tf_op jit(solution)/shard_map/all_to_all | solution.py:139
  227.3 33.6 %all-to-all-start.6 = ((f32[32,16,8,128]{3,1,2,0:T(8,128)}), f32[32,16,8,128]{3,1,2,0:T(8,128)}, u32[]{:S(2)}, u32[]{:S(2)}) async-start(f32[32,16,8,128]{3,1,2,0:T(8,128)} %copy.39), calls=%async_computation.6 | async-start | bytes 4194304 | tf_op jit(solution)/shard_map/all_to_all | solution.py:139
  234.4 28.8 %copy-start.1 = (f32[32,16,8,128]{3,2,0,1:T(8,128)S(1)}, f32[32,16,8,128]{3,2,0,1:T(8,128)}, u32[]{:S(2)}) copy-start(f32[32,16,8,128]{3,2,0,1:T(8,128)} %copy.69) | copy-start | bytes 6291460
Sparse Core Ops, SparseCore 0:
  90.4 62.9 all-gather.1

commit v6 on v2

--- a/solution.py
+++ b/solution.py
@@ -1,7 +1,9 @@
 import jax
 import jax.numpy as jnp
 from jax import lax
-from jax.sharding import PartitionSpec as P
+from jax.sharding import Mesh, PartitionSpec as P
+
+PIX = ("px", "pz", "pc")
 from jax.experimental import pallas as pl
 
 SUBSPACE = 2
@@ -96,17 +98,17 @@
 def shards(flats, projections, start_basis):
     frames_here, rows_dev, cols_dev = flats.shape
     ang_count = lax.axis_size("ang")
-    pix_count = lax.axis_size("pix")
+    pix_count = lax.psum(1, PIX)
     npix = rows_dev * cols_dev * ang_count * pix_count
     angle_count, rows_all, cols_here = projections.shape
 
     tiles_in = projections.reshape(angle_count, pix_count, rows_dev, cols_here).transpose(1, 0, 2, 3)
-    tiles = lax.all_to_all(tiles_in, "pix", 0, 0, tiled=True)
+    tiles = lax.all_to_all(tiles_in, PIX, 0, 0, tiled=True)
 
     local_gram, mean_flat = frame_gram(flats)
     device_count = ang_count * pix_count
     gram_rows = local_gram.reshape(device_count, -1)
-    gram = sum_by_exchange(gram_rows, ("ang", "pix"), device_count).reshape(frames_here, frames_here) / npix
+    gram = sum_by_exchange(gram_rows, ("ang",) + PIX, device_count).reshape(frames_here, frames_here) / npix
     basis = start_basis
     for turn in range(SUBSPACE):
         basis = orthonormal(jnp.dot(gram, basis, precision=lax.Precision.HIGHEST))
@@ -127,18 +129,21 @@
     partial_value = jnp.einsum(
         "pjrc,rkpc->jk", centred_frames, eigen_blk, precision=lax.Precision.HIGH
     )
-    fit_rhs = sum_by_exchange(partial_value, "pix", pix_count) / npix
+    paired = lax.psum(partial_value, PIX[-1])
+    fit_rhs = sum_by_exchange(paired, PIX[:-1], pix_count // 2) / npix
     weights = solve_normal(normal, fit_rhs)
     estimate = mean_blk.transpose(1, 0, 2)[:, None] + jnp.einsum(
         "jk,rkpc->pjrc", weights, eigen_blk, precision=lax.Precision.HIGH
     )
     tiles_out = tiles / jnp.maximum(estimate, floor_value)
-    back = lax.all_to_all(tiles_out, "pix", 0, 0, tiled=True)
+    back = lax.all_to_all(tiles_out, PIX, 0, 0, tiled=True)
     result = back.transpose(1, 0, 2, 3).reshape(angle_count, rows_all, cols_here)
     return result
 
 
 def solution(mesh):
-    in_specs = (P(None, "pix", "ang"), P("ang", None, "pix"), P())
-    out_specs = P("ang", None, "pix")
-    return jax.shard_map(shards, mesh=mesh, in_specs=in_specs, out_specs=out_specs, check_vma=False)
+    devices = mesh.devices.reshape(mesh.shape["ang"], -1, 4, 2)
+    fine = Mesh(devices, ("ang",) + PIX)
+    in_specs = (P(None, PIX, "ang"), P("ang", None, PIX), P())
+    out_specs = P("ang", None, PIX)
+    return jax.shard_map(shards, mesh=fine, in_specs=in_specs, out_specs=out_specs, check_vma=False)

time: 263 us -> 266 us (1.011)
  blocking collectives: 104 us -> 110 us
    psum x0 -> x1, blocking collectives: none -> 4.57 us  [shards(): paired = lax.psum(partial_value, PIX[-1])]
where the time goes in v6:
time: 266 us; the launch traced here: 265 us
  blocking collectives  110 us (41%)
  waiting for transfers between devices  44 us (17%)
  other arithmetic  29.2 us (11%)
  Pallas kernels  22.7 us (9%)
  matrix products  16.5 us (6%)
  starting transfers between devices  15.2 us (6%)
  local copies, waits for them, and re-layouts  13.8 us (5%)
  between operations  13.6 us (5%)
    all_to_all x1, blocking collectives, shards(): back = lax.all_to_all(tiles_out, PIX, 0, 0, tiled=True)  57.2 us
    all_to_all x1, waiting for transfers between devices, shards(): tiles = lax.all_to_all(tiles_in, PIX, 0, 0, tiled=True)  36.2 us
    all_to_all x1, blocking collectives, sum_by_exchange(): lax.all_to_all(rows.reshape(count, total // count, width), axes, 0, 0, ti...  22.2 us
    all_to_all x1, blocking collectives, sum_by_exchange(): gathered = lax.all_to_all(spread, axes, 0, 0, tiled=True)  15.2 us
    pallas_call x1, Pallas kernels, frame_gram(): pl.pallas_call(_gram_kernel, grid=(cols // width,), in_specs=[pl.BlockSpe...  13.7 us
    all_gather x1, blocking collectives, shards(): mean_rows = lax.all_gather(mean_flat, 'ang', axis=1, tiled=True)  11 us
    another operation x6, other arithmetic, orthonormal(): lower = jnp.linalg.cholesky(correlation)  10.1 us
    pallas_call x1, Pallas kernels, project_rows(): pl.pallas_call(_project_kernel, grid=(1,), in_specs=[pl.BlockSpec((m, k),...  8.96 us
  transfers between devices with their start and end apart: 4, of which 3 were waited for; matrix products, arithmetic and copies ran while one was open for 6% of the time, Pallas kernels for 0%

profile of v6, /device:TPU:1, one launch (start us, length us, event | category | flops | bytes accessed | tf_op | source)
XLA Modules:
  0.0 265.2 jit_solution(670809638991357840)
XLA Ops:
  6.5 0.0 copy-start
  6.5 0.0 all-gather.2.cloned.1.call-start
  6.5 13.7 %shard_map.37 = (f32[256,256]{1,0:T(8,128)}, f32[8,1024]{1,0:T(8,128)}) custom-call(f32[256,8,1024]{2,1,0:T(8,128)} %flats_ref.3), custom_call_target="tpu_custom_call" | custom-call | tf_op jit(solution)/shard_map/pallas_call | solution.py:57
  20.2 1.2 reshape_reshape.5
  21.5 22.2 %all_to_all.30 = f32[128,1,512]{2,1,0:T(1,128)S(1)} all-to-all(f32[128,1,512]{2,1,0:T(1,128)S(1)} %reshape_reshape.5), channel_id=1, replica_groups=mesh['ang'=4,'px'=4,'pz'=4,'pc'=2] {'ang','px','pz','pc'}, dimensions={0} | all-to-all | bytes 524288 | tf_op jit(solution)/shard_map/all_to_all | solution.py:28
  43.7 0.2 reduce_sum.18
  43.9 0.1 broadcast_in_dim.4
  44.1 15.2 %all_to_all.31 = f32[128,1,512]{2,1,0:T(1,128)S(1)} all-to-all(f32[128,1,512]{2,1,0:T(1,128)S(1)} %broadcast_in_dim.4), channel_id=1, replica_groups=mesh['ang'=4,'px'=4,'pz'=4,'pc'=2] {'ang','px','pz','pc'}, dimensions={0} | all-to-all | bytes 524288 | tf_op jit(solution)/shard_map/all_to_all | solution.py:31
  59.3 0.7 multiply_reduce_fusion
  60.0 0.0 copy-done
  60.1 0.4 fusion.28
  60.4 0.2 fusion.29
  60.6 0.1 copy.23
  60.7 4.4 %cholesky.59 = f32[48,48]{1,0:T(8,128)S(1)} custom-call(f32[48,48]{1,0:T(8,128)S(1)} %fusion.25), custom_call_target="Cholesky" | custom-call | tf_op jit(solution)/shard_map/jit(cholesky)/cholesky | solution.py:17
  65.1 0.6 compare_reduce_fusion.2
  65.8 0.7 fusion.15
  66.4 3.7 %custom-call.14 = f32[1,48,48]{1,2,0:T(8,128)S(1)} custom-call(f32[1,48,48]{2,1,0:T(8,128)S(1)} %fusion.15), custom_call_target="InvertDiagBlocksLowerTriangular" | custom-call | tf_op jit(solution)/shard_map/jit(_solve_triangular)/triangular_solve | solution.py:18
  70.1 0.2 fusion.13
  70.3 0.4 fusion.30
  70.7 0.2 fusion.31
  70.9 0.1 copy.24
  71.0 4.4 %cholesky.70 = f32[48,48]{1,0:T(8,128)S(1)} custom-call(f32[48,48]{1,0:T(8,128)S(1)} %fusion.23), custom_call_target="Cholesky" | custom-call | tf_op jit(solution)/shard_map/jit(cholesky)/cholesky | solution.py:17
  75.4 0.6 compare_reduce_fusion.1
  76.0 0.7 fusion.16
  76.7 3.7 %custom-call.15 = f32[1,48,48]{1,2,0:T(8,128)S(1)} custom-call(f32[1,48,48]{2,1,0:T(8,128)S(1)} %fusion.16), custom_call_target="InvertDiagBlocksLowerTriangular" | custom-call | tf_op jit(solution)/shard_map/jit(_solve_triangular)/triangular_solve | solution.py:18
  80.4 0.9 fusion.11.lhs_ref
  81.3 9.0 %shard_map.38 = f32[8,48,1024]{2,1,0:T(8,128)} custom-call(f32[48,256]{1,0:T(8,128)} %fusion.11.lhs_ref, f32[256,8,1024]{2,1,0:T(8,128)} %flats_ref.3, f32[8,1024]{1,0:T(8,128)} %get-tuple-element.9.mean_ref), custom_call_target="tpu_custom_call" | custom-call | tf_op jit(solution)/shard_map/pallas_call | solution.py:85
  90.2 0.0 all-gather.2.cloned.1.call-update
  90.2 6.6 %copy.20 = f32[32,32,8,128]{3,1,2,0:T(8,128)} copy(f32[32,32,8,128]{3,2,0,1:T(8,128)} %bitcast.93) | data formatting | bytes 8388608 | tf_op jit(solution)/shard_map/transpose | solution.py:105
  96.9 0.0 copy-start.2
  96.9 0.0 copy-start.1
  96.9 5.7 %all-to-all-start = ((f32[32,32,8,128]{3,1,2,0:T(8,128)}), f32[32,32,8,128]{3,1,2,0:T(8,128)}, u32[]{:S(2)}, u32[]{:S(2)}) async-start(f32[32,32,8,128]{3,1,2,0:T(8,128)} %copy.20), calls=%async_computation | async-start | bytes 8388608 | tf_op jit(solution)/shard_map/all_to_all | solution.py:106
  102.5 0.0 copy-done.2
  102.5 11.0 %all_gather.6 = f32[8,4096]{1,0:T(8,128)S(1)} all-gather(f32[8,1024]{1,0:T(8,128)S(1)} %copy-done.2), channel_id=1, replica_groups=mesh['ang'=4,'px'=4,'pz'=4,'pc'=2] {'ang'}, dimensions={1}, use_global_device_ids=true | all-gather | bytes 163840 | tf_op jit(solution)/shard_map/all_gather | solution.py:125
  113.5 0.0 copy-done.1
  113.6 0.4 fusion.32
  113.9 0.2 fusion.33
  114.1 0.1 copy.25
  114.2 4.4 %cholesky.81 = f32[48,48]{1,0:T(8,128)S(1)} custom-call(f32[48,48]{1,0:T(8,128)S(1)} %fusion.21), custom_call_target="Cholesky" | custom-call | tf_op jit(solution)/shard_map/jit(cholesky)/cholesky | solution.py:22
  118.6 36.2 %all-to-all-done = f32[32,32,8,128]{3,1,2,0:T(8,128)} async-done(((f32[32,32,8,128]{3,1,2,0:T(8,128)}), f32[32,32,8,128]{3,1,2,0:T(8,128)}, u32[]{:S(2)}, u32[]{:S(2)}) %all-to-all-start) | async-done | bytes 4194336 | tf_op jit(solution)/shard_map/all_to_all | solution.py:106
  154.8 0.0 all-gather.2.cloned.1.call-done
  154.8 6.9 %fusion = f32[32,48,1,1]{1,0,3,2:T(8,128)S(1)} fusion(f32[8,48,4096]{2,1,0:T(8,128)} %all-gather.2.cloned.1.call-done, f32[32,32,8,128]{3,1,2,0:T(8,128)} %all-to-all-done, f32[32,8,128]{2,0,1:T(8,128)S(1)} %copy.21), kind=kOutput, calls=%fused_computation | convolution fusion | flops 303038464 | bytes 10622976 | tf_op jit(solution)/shard_map/pjrc,rkpc->jk/dot_general | solution.py:129
  161.7 4.6 %psum.7 = f32[16,2,48]{2,1,0:T(2,128)} all-reduce(f32[16,2,48]{2,1,0:T(2,128)S(1)} %bitcast.95), channel_id=1, replica_groups=mesh['ang'=4,'px'=4,'pz'=4,'pc'=2] {'pc'}, use_global_device_ids=true, to_apply=%region_3.6 | all-reduce | flops 1536 | bytes 12288 | tf_op jit(solution)/shard_map/psum | solution.py:132
  166.3 6.0 %all-to-all-start.3 = ((f32[16,2,48]{2,1,0:T(2,128)}), f32[16,2,48]{2,1,0:T(2,128)S(1)}, u32[]{:S(2)}, u32[]{:S(2)}) async-start(f32[16,2,48]{2,1,0:T(2,128)} %psum.7), calls=%async_computation.3 | async-start | bytes 32768 | tf_op jit(solution)/shard_map/all_to_all | solution.py:28
  172.3 0.7 compare_reduce_fusion
  173.0 5.8 %all-to-all-done.3 = f32[16,2,48]{2,1,0:T(2,128)S(1)} async-done(((f32[16,2,48]{2,1,0:T(2,128)}), f32[16,2,48]{2,1,0:T(2,128)S(1)}, u32[]{:S(2)}, u32[]{:S(2)}) %all-to-all-start.3) | async-done | bytes 6176 | tf_op jit(solution)/shard_map/all_to_all | solution.py:28
  178.8 0.6 broadcast_in_dim.6
  179.4 3.5 %all-to-all-start.4 = ((f32[16,2,48]{2,1,0:T(2,128)}), f32[16,2,48]{2,1,0:T(2,128)S(1)}, u32[]{:S(2)}, u32[]{:S(2)}) async-start(f32[16,2,48]{2,1,0:T(2,128)} %broadcast_in_dim.6), calls=%async_computation.4 | async-start | bytes 32768 | tf_op jit(solution)/shard_map/all_to_all | solution.py:31
  182.9 0.7 fusion.17
  183.6 3.7 %custom-call.12 = f32[1,48,48]{1,2,0:T(8,128)S(1)} custom-call(f32[1,48,48]{2,1,0:T(8,128)S(1)} %fusion.17), custom_call_target="InvertDiagBlocksLowerTriangular" | custom-call | tf_op jit(solution)/shard_map/jit(_cho_solve)/triangular_solve | solution.py:23
  187.2 2.0 all-to-all-done.4
  189.3 0.1 fusion.19
  189.4 0.2 convolution_bitcast_fusion
  189.6 6.6 %fusion.7 = f32[32,32,8,128]{3,1,0,2:T(8,128)S(1)} fusion(f32[32,32,8,128]{3,1,2,0:T(8,128)} %all-to-all-done, f32[48,32,1,1]{0,1,3,2:T(8,128)S(1)} %convolution_bitcast_fusion, f32[32,8,128]{2,0,1:T(8,128)S(1)} %copy.21, f32[8,48,4096]{2,1,0:T(8,128)} %all-gather.2.cloned.1.call-done), kind=kOutput, calls=%fused_computation.8 | convolution fusion | flops 305135616 | bytes 14817280 | tf_op jit(solution)/shard_map/jk,rkpc->pjrc/dot_general | solution.py:135
  196.2 0.5 copy.31
  196.7 57.2 %all_to_all.32 = f32[32,32,8,128]{3,1,2,0:T(8,128)S(1)} all-to-all(f32[32,32,8,128]{3,1,2,0:T(8,128)S(1)} %copy.31), channel_id=1, replica_groups=mesh['ang'=4,'px'=4,'pz'=4,'pc'=2] {'px','pz','pc'}, dimensions={0} | all-to-all | bytes 8388608 | tf_op jit(solution)/shard_map/all_to_all | solution.py:139
  253.9 4.4 %copy.54 = f32[32,32,8,128]{3,2,0,1:T(8,128)} copy(f32[32,32,8,128]{3,1,2,0:T(8,128)S(1)} %all_to_all.32) | data formatting | bytes 8388608 | tf_op jit(solution)/shard_map/all_to_all | solution.py:139
  (10 shorter events, 0.2 us)
Async XLA Ops:
  6.5 53.5 %copy-start = (f32[256,48]{0,1:T(8,128)S(1)}, f32[256,48]{0,1:T(8,128)}, u32[]{:S(2)}) copy-start(f32[256,48]{0,1:T(8,128)} %param.8) | copy-start | bytes 147460
  6.5 148.3 %all-gather.2.cloned.1.call-start = ((), (), s32[]{:S(2)}) async-start(), calls=%async_computation.6 | async-start | bytes 7864320 | tf_op jit(solution)/shard_map/all_gather | solution.py:122
  96.9 5.7 %copy-start.2 = (f32[8,1024]{1,0:T(8,128)S(1)}, f32[8,1024]{1,0:T(8,128)}, u32[]{:S(2)}) copy-start(f32[8,1024]{1,0:T(8,128)} %get-tuple-element.9.mean_ref) | copy-start | bytes 98308
  96.9 16.7 %copy-start.1 = (f32[48,256]{1,0:T(8,128)S(1)}, f32[48,256]{1,0:T(8,128)}, u32[]{:S(2)}) copy-start(f32[48,256]{1,0:T(8,128)} %fusion.11.lhs_ref) | copy-start | bytes 147460
  96.9 57.9 %all-to-all-start = ((f32[32,32,8,128]{3,1,2,0:T(8,128)}), f32[32,32,8,128]{3,1,2,0:T(8,128)}, u32[]{:S(2)}, u32[]{:S(2)}) async-start(f32[32,32,8,128]{3,1,2,0:T(8,128)} %copy.20), calls=%async_computation | async-start | bytes 8388608 | tf_op jit(solution)/shard_map/all_to_all | solution.py:106
  166.3 12.5 %all-to-all-start.3 = ((f32[16,2,48]{2,1,0:T(2,128)}), f32[16,2,48]{2,1,0:T(2,128)S(1)}, u32[]{:S(2)}, u32[]{:S(2)}) async-start(f32[16,2,48]{2,1,0:T(2,128)} %psum.7), calls=%async_computation.3 | async-start | bytes 32768 | tf_op jit(solution)/shard_map/all_to_all | solution.py:28
  179.4 9.9 %all-to-all-start.4 = ((f32[16,2,48]{2,1,0:T(2,128)}), f32[16,2,48]{2,1,0:T(2,128)S(1)}, u32[]{:S(2)}, u32[]{:S(2)}) async-start(f32[16,2,48]{2,1,0:T(2,128)} %broadcast_in_dim.6), calls=%async_computation.4 | async-start | bytes 32768 | tf_op jit(solution)/shard_map/all_to_all | solution.py:31
Sparse Core Ops, SparseCore 0:
  90.4 62.9 all-gather.1

commit v7 on v2

--- a/solution.py
+++ b/solution.py
@@ -50,7 +50,7 @@
     gram_ref[...] = total
 
 
-def frame_gram(flats, width=256):
+def frame_gram(flats, width=128):
     frames, rows, cols = flats.shape
     return pl.pallas_call(
         _gram_kernel,

time: 263 us -> 268 us (1.019)
  Pallas kernels: 22.7 us -> 28.5 us
    pallas_call x1, Pallas kernels: 13.7 us -> 19.5 us  [frame_gram(): pl.pallas_call(_gram_kernel, grid=(cols // width,), in_specs=[pl.BlockSpe...]
where the time goes in v7:
time: 268 us
  blocking collectives  104 us (39%)
  waiting for transfers between devices  45 us (17%)
  other arithmetic  29.2 us (11%)
  Pallas kernels  28.5 us (11%)
  matrix products  17.1 us (6%)
  starting transfers between devices  16.9 us (6%)
  local copies, waits for them, and re-layouts  13.8 us (5%)
  between operations  13.6 us (5%)
    all_to_all x1, blocking collectives, shards(): back = lax.all_to_all(tiles_out, 'pix', 0, 0, tiled=True)  55.3 us
    all_to_all x1, waiting for transfers between devices, shards(): tiles = lax.all_to_all(tiles_in, 'pix', 0, 0, tiled=True)  36.2 us
    all_to_all x1, blocking collectives, sum_by_exchange(): lax.all_to_all(rows.reshape(count, total // count, width), axes, 0, 0, ti...  22.2 us
    pallas_call x1, Pallas kernels, frame_gram(): pl.pallas_call(_gram_kernel, grid=(cols // width,), in_specs=[pl.BlockSpe...  19.5 us
    all_to_all x1, blocking collectives, sum_by_exchange(): gathered = lax.all_to_all(spread, axes, 0, 0, tiled=True)  15.2 us
    all_gather x1, blocking collectives, shards(): mean_rows = lax.all_gather(mean_flat, 'ang', axis=1, tiled=True)  11 us
    another operation x6, other arithmetic, orthonormal(): lower = jnp.linalg.cholesky(correlation)  10.1 us
    pallas_call x1, Pallas kernels, project_rows(): pl.pallas_call(_project_kernel, grid=(1,), in_specs=[pl.BlockSpec((m, k),...  8.96 us
  transfers between devices with their start and end apart: 4, of which 3 were waited for; matrix products, arithmetic and copies ran while one was open for 6% of the time, Pallas kernels for 0%

profile of v7, /device:TPU:1, one launch (start us, length us, event | category | flops | bytes accessed | tf_op | source)
XLA Modules:
  0.0 267.9 jit_solution(2209605052264102928)
XLA Ops:
  6.5 0.0 copy-start
  6.5 0.0 all-gather.2.cloned.1.call-start
  6.5 19.5 %shard_map.37 = (f32[256,256]{1,0:T(8,128)}, f32[8,1024]{1,0:T(8,128)}) custom-call(f32[256,8,1024]{2,1,0:T(8,128)} %flats_ref.3), custom_call_target="tpu_custom_call" | custom-call | tf_op jit(solution)/shard_map/pallas_call | solution.py:55
  26.1 1.2 reshape_reshape.5
  27.3 22.2 %all_to_all.30 = f32[128,1,512]{2,1,0:T(1,128)S(1)} all-to-all(f32[128,1,512]{2,1,0:T(1,128)S(1)} %reshape_reshape.5), channel_id=1, replica_groups=mesh['ang'=4,'pix'=32] {'ang','pix'}, dimensions={0} | all-to-all | bytes 524288 | tf_op jit(solution)/shard_map/all_to_all | solution.py:26
  49.4 0.2 reduce_sum.18
  49.7 0.1 broadcast_in_dim.4
  49.8 15.2 %all_to_all.31 = f32[128,1,512]{2,1,0:T(1,128)S(1)} all-to-all(f32[128,1,512]{2,1,0:T(1,128)S(1)} %broadcast_in_dim.4), channel_id=1, replica_groups=mesh['ang'=4,'pix'=32] {'ang','pix'}, dimensions={0} | all-to-all | bytes 524288 | tf_op jit(solution)/shard_map/all_to_all | solution.py:29
  65.0 0.7 multiply_reduce_fusion
  65.8 0.0 copy-done
  65.8 0.4 fusion.28
  66.2 0.2 fusion.29
  66.4 0.1 copy.23
  66.4 4.4 %cholesky.59 = f32[48,48]{1,0:T(8,128)S(1)} custom-call(f32[48,48]{1,0:T(8,128)S(1)} %fusion.25), custom_call_target="Cholesky" | custom-call | tf_op jit(solution)/shard_map/jit(cholesky)/cholesky | solution.py:15
  70.9 0.6 compare_reduce_fusion.2
  71.5 0.7 fusion.15
  72.2 3.7 %custom-call.14 = f32[1,48,48]{1,2,0:T(8,128)S(1)} custom-call(f32[1,48,48]{2,1,0:T(8,128)S(1)} %fusion.15), custom_call_target="InvertDiagBlocksLowerTriangular" | custom-call | tf_op jit(solution)/shard_map/jit(_solve_triangular)/triangular_solve | solution.py:16
  75.8 0.2 fusion.13
  76.1 0.4 fusion.30
  76.5 0.2 fusion.31
  76.6 0.1 copy.24
  76.7 4.4 %cholesky.70 = f32[48,48]{1,0:T(8,128)S(1)} custom-call(f32[48,48]{1,0:T(8,128)S(1)} %fusion.23), custom_call_target="Cholesky" | custom-call | tf_op jit(solution)/shard_map/jit(cholesky)/cholesky | solution.py:15
  81.2 0.6 compare_reduce_fusion.1
  81.8 0.7 fusion.16
  82.5 3.7 %custom-call.15 = f32[1,48,48]{1,2,0:T(8,128)S(1)} custom-call(f32[1,48,48]{2,1,0:T(8,128)S(1)} %fusion.16), custom_call_target="InvertDiagBlocksLowerTriangular" | custom-call | tf_op jit(solution)/shard_map/jit(_solve_triangular)/triangular_solve | solution.py:16
  86.1 0.9 fusion.11.lhs_ref
  87.0 9.0 %shard_map.38 = f32[8,48,1024]{2,1,0:T(8,128)} custom-call(f32[48,256]{1,0:T(8,128)} %fusion.11.lhs_ref, f32[256,8,1024]{2,1,0:T(8,128)} %flats_ref.3, f32[8,1024]{1,0:T(8,128)} %get-tuple-element.9.mean_ref), custom_call_target="tpu_custom_call" | custom-call | tf_op jit(solution)/shard_map/pallas_call | solution.py:83
  96.0 0.0 all-gather.2.cloned.1.call-update
  96.0 6.6 %copy.20 = f32[32,32,8,128]{3,1,2,0:T(8,128)} copy(f32[32,32,8,128]{3,2,0,1:T(8,128)} %bitcast.95) | data formatting | bytes 8388608 | tf_op jit(solution)/shard_map/transpose | solution.py:103
  102.6 0.0 copy-start.2
  102.6 0.0 copy-start.1
  102.6 5.7 %all-to-all-start = ((f32[32,32,8,128]{3,1,2,0:T(8,128)}), f32[32,32,8,128]{3,1,2,0:T(8,128)}, u32[]{:S(2)}, u32[]{:S(2)}) async-start(f32[32,32,8,128]{3,1,2,0:T(8,128)} %copy.20), calls=%async_computation | async-start | bytes 8388608 | tf_op jit(solution)/shard_map/all_to_all | solution.py:104
  108.3 0.0 copy-done.2
  108.3 11.0 %all_gather.6 = f32[8,4096]{1,0:T(8,128)S(1)} all-gather(f32[8,1024]{1,0:T(8,128)S(1)} %copy-done.2), channel_id=1, replica_groups=mesh['ang'=4,'pix'=32] {'ang'}, dimensions={1}, use_global_device_ids=true | all-gather | bytes 163840 | tf_op jit(solution)/shard_map/all_gather | solution.py:123
  119.3 0.0 copy-done.1
  119.3 0.4 fusion.32
  119.7 0.2 fusion.33
  119.9 0.1 copy.25
  119.9 4.4 %cholesky.81 = f32[48,48]{1,0:T(8,128)S(1)} custom-call(f32[48,48]{1,0:T(8,128)S(1)} %fusion.21), custom_call_target="Cholesky" | custom-call | tf_op jit(solution)/shard_map/jit(cholesky)/cholesky | solution.py:20
  124.4 36.2 %all-to-all-done = f32[32,32,8,128]{3,1,2,0:T(8,128)} async-done(((f32[32,32,8,128]{3,1,2,0:T(8,128)}), f32[32,32,8,128]{3,1,2,0:T(8,128)}, u32[]{:S(2)}, u32[]{:S(2)}) %all-to-all-start) | async-done | bytes 4194336 | tf_op jit(solution)/shard_map/all_to_all | solution.py:104
  160.6 0.0 all-gather.2.cloned.1.call-done
  160.6 7.5 %fusion = f32[32,48,1,1]{1,0,3,2:T(8,128)} fusion(f32[8,48,4096]{2,1,0:T(8,128)} %all-gather.2.cloned.1.call-done, f32[32,32,8,128]{3,1,2,0:T(8,128)} %all-to-all-done, f32[32,8,128]{2,0,1:T(8,128)S(1)} %copy.21), kind=kOutput, calls=%fused_computation | convolution fusion | flops 303038464 | bytes 10622976 | tf_op jit(solution)/shard_map/pjrc,rkpc->jk/dot_general | solution.py:127
  168.0 7.1 %all-to-all-start.3 = ((f32[32,1,48]{2,1,0:T(1,128)}), f32[32,1,48]{2,1,0:T(1,128)S(1)}, u32[]{:S(2)}, u32[]{:S(2)}) async-start(f32[32,1,48]{2,1,0:T(1,128)} %bitcast.18), calls=%async_computation.3 | async-start | bytes 32768 | tf_op jit(solution)/shard_map/all_to_all | solution.py:26
  175.2 0.7 compare_reduce_fusion
  175.9 6.2 %all-to-all-done.3 = f32[32,1,48]{2,1,0:T(1,128)S(1)} async-done(((f32[32,1,48]{2,1,0:T(1,128)}), f32[32,1,48]{2,1,0:T(1,128)S(1)}, u32[]{:S(2)}, u32[]{:S(2)}) %all-to-all-start.3) | async-done | bytes 6176 | tf_op jit(solution)/shard_map/all_to_all | solution.py:26
  182.1 0.1 reduce_sum.19
  182.1 0.6 broadcast_in_dim.6
  182.7 4.1 %all-to-all-start.4 = ((f32[32,1,48]{2,1,0:T(1,128)}), f32[32,1,48]{2,1,0:T(1,128)S(1)}, u32[]{:S(2)}, u32[]{:S(2)}) async-start(f32[32,1,48]{2,1,0:T(1,128)} %broadcast_in_dim.6), calls=%async_computation.4 | async-start | bytes 32768 | tf_op jit(solution)/shard_map/all_to_all | solution.py:29
  186.9 0.7 fusion.17
  187.5 3.7 %custom-call.12 = f32[1,48,48]{1,2,0:T(8,128)S(1)} custom-call(f32[1,48,48]{2,1,0:T(8,128)S(1)} %fusion.17), custom_call_target="InvertDiagBlocksLowerTriangular" | custom-call | tf_op jit(solution)/shard_map/jit(_cho_solve)/triangular_solve | solution.py:21
  191.2 2.6 all-to-all-done.4
  193.9 0.1 fusion.19
  194.0 0.2 convolution_bitcast_fusion
  194.2 6.6 %fusion.7 = f32[32,32,8,128]{3,1,0,2:T(8,128)S(1)} fusion(f32[32,32,8,128]{3,1,2,0:T(8,128)} %all-to-all-done, f32[48,32,1,1]{0,1,3,2:T(8,128)S(1)} %convolution_bitcast_fusion, f32[32,8,128]{2,0,1:T(8,128)S(1)} %copy.21, f32[8,48,4096]{2,1,0:T(8,128)} %all-gather.2.cloned.1.call-done), kind=kOutput, calls=%fused_computation.8 | convolution fusion | flops 305135616 | bytes 14817280 | tf_op jit(solution)/shard_map/jk,rkpc->pjrc/dot_general | solution.py:132
  200.8 0.5 copy.32
  201.3 55.3 %all_to_all.32 = f32[32,32,8,128]{3,1,2,0:T(8,128)S(1)} all-to-all(f32[32,32,8,128]{3,1,2,0:T(8,128)S(1)} %copy.32), channel_id=1, replica_groups=mesh['ang'=4,'pix'=32] {'pix'}, dimensions={0} | all-to-all | bytes 8388608 | tf_op jit(solution)/shard_map/all_to_all | solution.py:136
  256.6 4.4 %copy.55 = f32[32,32,8,128]{3,2,0,1:T(8,128)} copy(f32[32,32,8,128]{3,1,2,0:T(8,128)S(1)} %all_to_all.32) | data formatting | bytes 8388608 | tf_op jit(solution)/shard_map/all_to_all | solution.py:136
  (9 shorter events, 0.2 us)
Async XLA Ops:
  6.5 59.3 %copy-start = (f32[256,48]{0,1:T(8,128)S(1)}, f32[256,48]{0,1:T(8,128)}, u32[]{:S(2)}) copy-start(f32[256,48]{0,1:T(8,128)} %param.8) | copy-start | bytes 147460
  6.5 154.0 %all-gather.2.cloned.1.call-start = ((), (), s32[]{:S(2)}) async-start(), calls=%async_computation.6 | async-start | bytes 7864320 | tf_op jit(solution)/shard_map/all_gather | solution.py:120
  102.6 5.7 %copy-start.2 = (f32[8,1024]{1,0:T(8,128)S(1)}, f32[8,1024]{1,0:T(8,128)}, u32[]{:S(2)}) copy-start(f32[8,1024]{1,0:T(8,128)} %get-tuple-element.9.mean_ref) | copy-start | bytes 98308
  102.6 16.7 %copy-start.1 = (f32[48,256]{1,0:T(8,128)S(1)}, f32[48,256]{1,0:T(8,128)}, u32[]{:S(2)}) copy-start(f32[48,256]{1,0:T(8,128)} %fusion.11.lhs_ref) | copy-start | bytes 147460
  102.6 57.9 %all-to-all-start = ((f32[32,32,8,128]{3,1,2,0:T(8,128)}), f32[32,32,8,128]{3,1,2,0:T(8,128)}, u32[]{:S(2)}, u32[]{:S(2)}) async-start(f32[32,32,8,128]{3,1,2,0:T(8,128)} %copy.20), calls=%async_computation | async-start | bytes 8388608 | tf_op jit(solution)/shard_map/all_to_all | solution.py:104
  168.0 14.0 %all-to-all-start.3 = ((f32[32,1,48]{2,1,0:T(1,128)}), f32[32,1,48]{2,1,0:T(1,128)S(1)}, u32[]{:S(2)}, u32[]{:S(2)}) async-start(f32[32,1,48]{2,1,0:T(1,128)} %bitcast.18), calls=%async_computation.3 | async-start | bytes 32768 | tf_op jit(solution)/shard_map/all_to_all | solution.py:26
  182.7 11.1 %all-to-all-start.4 = ((f32[32,1,48]{2,1,0:T(1,128)}), f32[32,1,48]{2,1,0:T(1,128)S(1)}, u32[]{:S(2)}, u32[]{:S(2)}) async-start(f32[32,1,48]{2,1,0:T(1,128)} %broadcast_in_dim.6), calls=%async_computation.4 | async-start | bytes 32768 | tf_op jit(solution)/shard_map/all_to_all | solution.py:29
Sparse Core Ops, SparseCore 0:
  96.1 62.9 all-gather.1
